TPU v7x, 512 devices: a whole 4x8x8 slice. The times are simulated.
512 devices in a mesh: blk: 16 (over x_lo, y), exp: 32 (over z, x_hi, core).
Axes of the slice: x: 4 (x_hi: 2, x_lo: 2; x = x_hi * 2 + x_lo), y: 8, z: 8, core: 2. Of those that a mesh axis runs over, the one named last changes fastest.
Arguments:
- residual: bfloat16 [32, 2048, 1024], P('exp', 'blk'), may hold values from -6 to 6
- queries: bfloat16 [32, 2048, 1024], P('exp', 'blk'), may hold values from -6 to 6
- suffix_kv: bfloat16 [32, 2048, 1024], P('exp', 'blk'), may hold values from -6 to 6
- prompt_kv: bfloat16 [32, 1024, 1024], P('exp', 'blk'), may hold values from -6 to 6
- prompt_lengths: int32 [32], P('exp'), may hold values from 1 to 1024, as said below
- block_keep: int32 [32, 32], P('exp', 'blk'), may hold values 0 or 1
- suffix_lengths: int32 [32, 16, 4], P('exp', 'blk'), may hold values from 1 to 64, 128 in all within a row
- out_weight: bfloat16 [1024, 1024], P('exp'), may hold values from -0.75 to 0.75
- routes: int32 [32, 2048, 8], P('exp', 'blk'), may hold values from 0 to 31, all different within a row; in each aligned block of 128 rows (0 to 127, 128 to 255, ..., all dimensions but the last counted through in order) at most 40 rows name the same one
- route_weight: float32 [32, 2048, 8], P('exp', 'blk'), may hold values from 0.02 to 0.25
- gate_up_weight: bfloat16 [32, 1024, 1024], P('exp'), may hold values from -0.1875 to 0.1875
- down_weight: bfloat16 [32, 512, 1024], P('exp'), may hold values from -0.25 to 0.25
- page_owner: int32 [32, 128, 1], P('exp', 'blk'), may hold values from 0 to 15; in each aligned block of 8 rows (0 to 7, 8 to 15, ..., all dimensions but the last counted through in order) at most 2 rows name the same one
Outputs:
- attended: bfloat16 [32, 2048, 1024], P('exp', 'blk')
- layer_out: bfloat16 [32, 2048, 1024], P('exp', 'blk')
- cache_pages: bfloat16 [32, 4096, 1024], P('exp', 'blk')
Inputs may be any that keep to these rules, and one draw needn't show every extreme that they name: `prompt_lengths`: some group's prompt length equals 1024. `suffix_lengths`: each device's 4 request lengths sum to 128. `routes`: each token names 8 different experts; among the tokens of one device at most 40 name any one expert, and that bound is reached. `page_owner`: among the 8 pages of one device at most 2 go to any one owner, and that bound is reached.
All inputs are finite; a program needn't handle non-finite values. No bound on the sum of `block_keep` on one device may be relied on, other than what follows from the above.
Results may differ from a plain program's by a relative error of at most 0.013.
Values may be sent and summed in bfloat16 or wider, within the bound.
No kernel may reach another device: no remote copies, remote signals or barrier semaphores. Data moves between devices by JAX's collectives and lax.ppermute only.
A program may use at most 64 MiB of HBM per device.

v0:
```python
import jax
import jax.numpy as jnp
from jax import lax
from jax.sharding import PartitionSpec as P

D = 1024
H = 16
KVH = 8
HD = 64
FF = 512
TOPK = 8
EXP_DEV = 1
KB = 32
PAGE = 8


SCALE = 0.125
NEGATIVE = -1e30
EPSILON = 1e-06


def segment_of(lengths, count):
    ends = jnp.cumsum(lengths)
    position = jnp.arange(count, dtype=jnp.int32)
    return jnp.sum((position[:, None] >= ends[None, :]).astype(jnp.int32), axis=1)


def rank_within(labels, count):
    onehot = (labels[:, None] == jnp.arange(count, dtype=jnp.int32)[None, :]).astype(jnp.int32)
    before = jnp.cumsum(onehot, axis=0) - onehot
    return jnp.sum(before * onehot, axis=1)


def absorb(carry_state, query_heads, key_heads, value_heads, visible):
    running_max, denom, numerator = carry_state
    scores = (
        jnp.einsum("tkgd,skd->tkgs", query_heads, key_heads, preferred_element_type=jnp.float32)
        * SCALE
    )
    new_max = jnp.maximum(running_max, jnp.max(jnp.where(visible, scores, NEGATIVE), axis=-1))
    factor = jnp.exp(running_max - new_max)
    weight = jnp.where(visible, jnp.exp(scores - new_max[..., None]), 0.0)
    denom = denom * factor + jnp.sum(weight, axis=-1)
    added = jnp.einsum(
        "tkgs,skd->tkgd",
        weight.astype(jnp.bfloat16),
        value_heads,
        preferred_element_type=jnp.float32,
    )
    numerator = numerator * factor[..., None] + added
    return (new_max, denom, numerator)


def local(
    residual,
    queries,
    suffix_kv,
    prompt_kv,
    prompt_lengths,
    block_keep,
    suffix_lengths,
    out_weight,
    routes,
    route_weight,
    gate_up_weight,
    down_weight,
    page_owner,
):
    tok_rows = queries.shape[1]
    kv_width = suffix_kv.shape[2] // 2
    group_size = H // KVH
    query_heads = queries[0].reshape(tok_rows, KVH, group_size, HD)
    own_keys = suffix_kv[0, :, :kv_width].reshape(tok_rows, KVH, HD)
    own_values = suffix_kv[0, :, kv_width:].reshape(tok_rows, KVH, HD)
    segment = segment_of(suffix_lengths[0, 0], tok_rows)
    position = jnp.arange(tok_rows, dtype=jnp.int32)
    own_seen = ((segment[:, None] == segment[None, :]) & (position[None, :] <= position[:, None]))[
        :, None, None, :
    ]
    start_state = (
        jnp.full((tok_rows, KVH, group_size), NEGATIVE, jnp.float32),
        jnp.zeros((tok_rows, KVH, group_size), jnp.float32),
        jnp.zeros((tok_rows, KVH, group_size, HD), jnp.float32),
    )
    carry_state = absorb(start_state, query_heads, own_keys, own_values, own_seen)
    block_rows = prompt_kv.shape[1]
    keep_rows = jnp.repeat(block_keep[0], KB)
    position_abs = lax.axis_index("blk") * block_rows + jnp.arange(block_rows, dtype=jnp.int32)
    live_keys = ((keep_rows > 0) & (position_abs < prompt_lengths[0])).astype(jnp.int32)[None, :]
    piece_kv = lax.all_gather(prompt_kv, "blk", axis=1, tiled=True)
    piece_live = lax.all_gather(live_keys, "blk", axis=1, tiled=True)
    count = piece_kv.shape[1]
    key_heads = piece_kv[0, :, :kv_width].reshape(count, KVH, HD)
    value_heads = piece_kv[0, :, kv_width:].reshape(count, KVH, HD)
    visible = (piece_live[0] > 0)[None, None, None, :]
    running_max, denom, numerator = absorb(
        carry_state, query_heads, key_heads, value_heads, visible
    )
    attended = (numerator / denom[..., None]).reshape(tok_rows, H * HD).astype(jnp.bfloat16)
    projected = jnp.dot(
        attended,
        lax.all_gather(out_weight, "exp", axis=0, tiled=True),
        preferred_element_type=jnp.float32,
    )
    stream = (residual[0].astype(jnp.float32) + projected).astype(jnp.bfloat16)
    stream_f32 = stream.astype(jnp.float32)
    normed = (
        stream_f32 * lax.rsqrt(jnp.mean(stream_f32 * stream_f32, axis=-1, keepdims=True) + EPSILON)
    ).astype(jnp.bfloat16)
    exp_count = lax.axis_size("exp")
    experts = EXP_DEV * exp_count
    capacity = min(tok_rows, 5 * tok_rows * TOPK // (4 * experts))
    flat_routes = routes[0].reshape(-1)
    slot_index = flat_routes * capacity + rank_within(flat_routes, experts)
    dispatch = (
        jnp.zeros((experts * capacity, D), jnp.bfloat16)
        .at[slot_index]
        .set(jnp.repeat(normed, TOPK, axis=0))
    )
    dispatch = dispatch.reshape(experts, capacity, D)
    arrived = lax.all_to_all(dispatch, "exp", split_axis=0, concat_axis=0, tiled=True)
    count = arrived.shape[1]
    grouped = arrived.reshape(exp_count, EXP_DEV, count, D)
    picked_rows = grouped[:, 0].reshape(exp_count * count, D)
    gate_up = jnp.dot(picked_rows, gate_up_weight[0], preferred_element_type=jnp.float32)
    hidden = (jax.nn.silu(gate_up[:, :FF]) * gate_up[:, FF:]).astype(jnp.bfloat16)
    result = jnp.dot(hidden, down_weight[0], preferred_element_type=jnp.float32).astype(
        jnp.bfloat16
    )
    results = [result.reshape(exp_count, count, D)]
    outgoing = jnp.stack(results, axis=1).reshape(exp_count * EXP_DEV, count, D)
    returned = lax.all_to_all(outgoing, "exp", split_axis=0, concat_axis=0, tiled=True)
    picked = (
        returned.reshape(experts * capacity, D)[slot_index]
        .astype(jnp.float32)
        .reshape(tok_rows, TOPK, D)
    )
    layer_out = (stream_f32 + jnp.sum(picked * route_weight[0][:, :, None], axis=1)).astype(
        jnp.bfloat16
    )
    page_count = block_rows // PAGE
    blk_count = lax.axis_size("blk")
    page_capacity = max(2, 2 * page_count // blk_count)
    page_rows = prompt_kv[0].reshape(page_count, PAGE, 2 * kv_width)
    owners = page_owner[0, :, 0]
    page_slot = owners * page_capacity + rank_within(owners, blk_count)
    outgoing_pages = (
        jnp.zeros((blk_count * page_capacity, PAGE, 2 * kv_width), jnp.bfloat16)
        .at[page_slot]
        .set(page_rows)
    )
    arrived_pages = lax.all_to_all(outgoing_pages, "blk", split_axis=0, concat_axis=0, tiled=True)
    cache_pages = arrived_pages.reshape(1, blk_count * page_capacity * PAGE, 2 * kv_width)
    return (attended[None], layer_out[None], cache_pages)


def solution(mesh):
    return jax.shard_map(
        local,
        mesh=mesh,
        in_specs=(
            P("exp", "blk", None),
            P("exp", "blk", None),
            P("exp", "blk", None),
            P("exp", "blk", None),
            P("exp"),
            P("exp", "blk"),
            P("exp", "blk", None),
            P("exp", None),
            P("exp", "blk", None),
            P("exp", "blk", None),
            P("exp", None, None),
            P("exp", None, None),
            P("exp", "blk", None),
        ),
        out_specs=(P("exp", "blk", None), P("exp", "blk", None), P("exp", "blk", None)),
        check_vma=False,
    )
```

profile of v0, /device:TPU:1, one launch (start us, length us, event | category | flops | bytes accessed | tf_op | source)
XLA Modules:
  0.0 363.6 jit_solution(11211758966048198514)
XLA Ops:
  9.4 0.8 copy.48
  11.6 1.0 fusion.51
  12.7 0.8 reduce-window.18
  13.6 9.0 %reduce-window.19 = s32[32,8,128]{2,1,0:T(8,128)S(1)} reduce-window(s32[32,8,128]{2,1,0:T(8,128)S(1)} %fusion.39, s32[]{:T(128)} %constant.17.clone.1), window={size=1x1x128 pad=0_0x0_0x127_0}, to_apply=%region_6.7 | reduce-window | flops 4161536 | bytes 262148 | tf_op jit(solution)/shard_map/reduce-window.1
  23.0 1.3 dynamic-slice
  25.2 1.1 copy.41
  26.8 15.1 %all-reduce = s32[1024]{0:T(1024)S(1)} all-reduce(s32[1024]{0:T(1024)S(1)} %fusion.43), channel_id=1, replica_groups=mesh['blk'=16,'exp'=32] {'blk'}, use_global_device_ids=true, to_apply=%add | all-reduce | flops 1024 | bytes 8192
  43.3 1.9 select_reduce_fusion
  45.2 35.0 %all-gather.3.cloned.1.call-done = bf16[1,1024,1024]{2,1,0:T(8,128)(2,1)} async-done(((bf16[1,64,1024]{2,1,0:T(8,128)(2,1)}), bf16[1,1024,1024]{2,1,0:T(8,128)(2,1)}) %all-gather.3.cloned.1.call-update) | async-done | bytes 2097168 | tf_op jit(solution)/shard_map/all_gather | solution.py:90
  80.2 2.7 fusion.50
  82.9 1.3 copy.45
  84.2 1.5 copy.44
  85.7 2.9 fusion
  89.0 2.2 fusion.3
  91.2 1.5 fusion.17
  93.1 84.1 %all-gather.5.cloned.1.call-done = bf16[1024,1024]{1,0:T(8,128)(2,1)} async-done(((bf16[32,1024]{1,0:T(8,128)(2,1)}), bf16[1024,1024]{1,0:T(8,128)(2,1)}) %all-gather.5.cloned.1.call-update) | async-done | bytes 2097168 | tf_op jit(solution)/shard_map/all_gather | solution.py:102
  177.2 2.1 multiply_reduce_fusion
  179.5 7.1 %scatter_custom_fusion = bf16[1280,1024]{1,0:T(8,128)(2,1)} fusion(s32[1024]{0:T(1024)S(1)} %bitcast.143, bf16[]{:T(256)} %constant.12.clone.1, bf16[128,1024]{1,0:T(8,128)(2,1)S(1)} %multiply_convert_fusion), kind=kCustom, calls=%fused_computation.19 | custom fusion | bytes 2883586 | tf_op jit(solution)/shard_map/scatter | solution.py:118
  186.6 4.8 %all-to-all-start = ((bf16[32,40,1024]{2,1,0:T(8,128)(2,1)}), bf16[32,40,1024]{2,1,0:T(8,128)(2,1)}, u32[]{:S(2)}, u32[]{:S(2)}) async-start(bf16[32,40,1024]{2,1,0:T(8,128)(2,1)} %bitcast.128), calls=%async_computation | async-start | bytes 5242880 | tf_op jit(solution)/shard_map/all_to_all | solution.py:121
  191.7 0.9 broadcast_in_dim.91
  192.5 2.1 scatter_fusion
  194.6 57.8 %all-to-all-done = bf16[32,40,1024]{2,1,0:T(8,128)(2,1)} async-done(((bf16[32,40,1024]{2,1,0:T(8,128)(2,1)}), bf16[32,40,1024]{2,1,0:T(8,128)(2,1)}, u32[]{:S(2)}, u32[]{:S(2)}) %all-to-all-start) | async-done | bytes 2621472 | tf_op jit(solution)/shard_map/all_to_all | solution.py:121
  252.4 7.4 %all-to-all-start.2 = ((bf16[32,8,1024]{2,1,0:T(8,128)(2,1)}), bf16[32,8,1024]{2,1,0:T(8,128)(2,1)S(1)}, u32[]{:S(2)}, u32[]{:S(2)}) async-start(bf16[32,8,1024]{2,1,0:T(8,128)(2,1)} %scatter_fusion), calls=%async_computation.2 | async-start | bytes 1048576 | tf_op jit(solution)/shard_map/all_to_all | solution.py:152
  259.8 4.7 %fusion.10 = f32[1280,1024]{1,0:T(8,128)S(1)} fusion(bf16[1280,1024]{1,0:T(8,128)(2,1)} %bitcast.32, bf16[1,1024,1024]{2,1,0:T(8,128)(2,1)S(1)} %copy-done), kind=kOutput, calls=%fused_computation.17 | convolution fusion | flops 2684354560 | bytes 9961472 | tf_op jit(solution)/shard_map/dot_general | solution.py:125
  264.6 3.1 convolution_convert_fusion
  267.7 5.3 %all-to-all-done.2 = bf16[32,8,1024]{2,1,0:T(8,128)(2,1)S(1)} async-done(((bf16[32,8,1024]{2,1,0:T(8,128)(2,1)}), bf16[32,8,1024]{2,1,0:T(8,128)(2,1)S(1)}, u32[]{:S(2)}, u32[]{:S(2)}) %all-to-all-start.2) | async-done | bytes 524320 | tf_op jit(solution)/shard_map/all_to_all | solution.py:152
  273.0 10.2 %all-to-all-start.1 = ((bf16[32,40,1024]{2,1,0:T(8,128)(2,1)}), bf16[32,40,1024]{2,1,0:T(8,128)(2,1)}, u32[]{:S(2)}, u32[]{:S(2)}) async-start(bf16[32,40,1024]{2,1,0:T(8,128)(2,1)} %bitcast.130), calls=%async_computation.1 | async-start | bytes 5242880 | tf_op jit(solution)/shard_map/all_to_all | solution.py:132
  283.3 0.9 copy.53
  284.1 60.0 %all-to-all-done.1 = bf16[32,40,1024]{2,1,0:T(8,128)(2,1)} async-done(((bf16[32,40,1024]{2,1,0:T(8,128)(2,1)}), bf16[32,40,1024]{2,1,0:T(8,128)(2,1)}, u32[]{:S(2)}, u32[]{:S(2)}) %all-to-all-start.1) | async-done | bytes 2621472 | tf_op jit(solution)/shard_map/all_to_all | solution.py:132
  344.2 8.1 %gather_fusion = bf16[1024,1024]{1,0:T(8,128)(2,1)} fusion(bf16[1280,1024]{1,0:T(8,128)(2,1)} %bitcast.36, s32[1024]{0:T(1024)S(1)} %broadcast_clamp_fusion), kind=kCustom, calls=%fused_computation | custom fusion | bytes 4198400 | tf_op jit(solution)/shard_map/gather | solution.py:134
  352.3 2.9 fusion.5
  356.0 0.8 copy.66
  (63 shorter events, 7.4 us)
Async XLA Ops:
  7.2 252.6 %copy-start = (bf16[1,1024,1024]{2,1,0:T(8,128)(2,1)S(1)}, bf16[1,1024,1024]{2,1,0:T(8,128)(2,1)}, u32[]{:S(2)}) copy-start(bf16[1,1024,1024]{2,1,0:T(8,128)(2,1)} %param.23) | copy-start | bytes 6291460
  7.2 73.0 %all-gather.3.cloned.1.call-start = ((), (), s32[]{:S(2)}) async-start(), calls=%async_computation.3 | async-start | bytes 2228224 | tf_op jit(solution)/shard_map/all_gather | solution.py:90
  7.9 169.3 %all-gather.5.cloned.1.call-start = ((), (), s32[]{:S(2)}) async-start(), calls=%async_computation.4 | async-start | bytes 2162688 | tf_op jit(solution)/shard_map/all_gather | solution.py:102
  85.7 3.0 copy-start.5
  85.7 3.0 copy-start.1
  85.7 3.2 copy-start.7
  88.9 2.2 copy-start.2
  92.7 84.5 %copy-start.4 = (bf16[1,128,1024]{2,1,0:T(8,128)(2,1)S(1)}, bf16[1,128,1024]{2,1,0:T(8,128)(2,1)}, u32[]{:S(2)}) copy-start(bf16[1,128,1024]{2,1,0:T(8,128)(2,1)} %param.13) | copy-start | bytes 786436
  93.0 86.4 %copy-start.6 = (s32[1024,1]{0,1:T(1,128)S(1)}, s32[1024,1]{0,1:T(1,128)}, u32[]{:S(2)}) copy-start(s32[1024,1]{0,1:T(1,128)} %compare_select_fusion) | copy-start | bytes 12292
  186.6 4.8 %copy-start.9 = (s32[1,8,1]{1,2,0:T(1,128)S(1)}, s32[1,8,1]{1,2,0:T(1,128)}, u32[]{:S(2)}) copy-start(s32[1,8,1]{1,2,0:T(1,128)} %param.25) | copy-start | bytes 100
  186.6 5.9 %copy-start.3 = (bf16[1,64,1024]{2,1,0:T(8,128)(2,1)S(1)}, bf16[1,64,1024]{2,1,0:T(8,128)(2,1)}, u32[]{:S(2)}) copy-start(bf16[1,64,1024]{2,1,0:T(8,128)(2,1)} %param.16) | copy-start | bytes 393220
  186.6 65.8 %all-to-all-start = ((bf16[32,40,1024]{2,1,0:T(8,128)(2,1)}), bf16[32,40,1024]{2,1,0:T(8,128)(2,1)}, u32[]{:S(2)}, u32[]{:S(2)}) async-start(bf16[32,40,1024]{2,1,0:T(8,128)(2,1)} %bitcast.128), calls=%async_computation | async-start | bytes 5242880 | tf_op jit(solution)/shard_map/all_to_all | solution.py:121
  252.4 20.6 %all-to-all-start.2 = ((bf16[32,8,1024]{2,1,0:T(8,128)(2,1)}), bf16[32,8,1024]{2,1,0:T(8,128)(2,1)S(1)}, u32[]{:S(2)}, u32[]{:S(2)}) async-start(bf16[32,8,1024]{2,1,0:T(8,128)(2,1)} %scatter_fusion), calls=%async_computation.2 | async-start | bytes 1048576 | tf_op jit(solution)/shard_map/all_to_all | solution.py:152
  259.8 4.8 %copy-start.10 = (bf16[1,512,1024]{2,1,0:T(8,128)(2,1)S(1)}, bf16[1,512,1024]{2,1,0:T(8,128)(2,1)}, u32[]{:S(2)}) copy-start(bf16[1,512,1024]{2,1,0:T(8,128)(2,1)} %param.24) | copy-start | bytes 3145732
  273.0 10.2 %copy-start.8 = (f32[1,128,8]{1,2,0:T(8,128)S(1)}, f32[1,128,8]{1,2,0:T(8,128)}, u32[]{:S(2)}) copy-start(f32[1,128,8]{1,2,0:T(8,128)} %param.22) | copy-start | bytes 12292
  273.0 71.2 %all-to-all-start.1 = ((bf16[32,40,1024]{2,1,0:T(8,128)(2,1)}), bf16[32,40,1024]{2,1,0:T(8,128)(2,1)}, u32[]{:S(2)}, u32[]{:S(2)}) async-start(bf16[32,40,1024]{2,1,0:T(8,128)(2,1)} %bitcast.130), calls=%async_computation.1 | async-start | bytes 5242880 | tf_op jit(solution)/shard_map/all_to_all | solution.py:132
Sparse Core Ops, SparseCore 0:
  10.1 70.0 all-gather.2
  83.6 93.5 all-gather.4
where the time goes:
time: 364 us
  waiting for transfers between devices  244 us (67%)
  local copies, waits for them, and re-layouts  30.7 us (8%)
  starting transfers between devices  22.4 us (6%)
  other arithmetic  19.4 us (5%)
  matrix products  16.7 us (5%)
  between operations  15.7 us (4%)
  blocking collectives  15.1 us (4%)
    all_gather x1, waiting for transfers between devices, local(): lax.all_gather(out_weight, 'exp', axis=0, tiled=True)  84.1 us
    all_to_all x1, waiting for transfers between devices, local(): lax.all_to_all(outgoing, 'exp', split_axis=0, concat_axis=0, tiled=True)  60 us
    all_to_all x1, waiting for transfers between devices, local(): lax.all_to_all(dispatch, 'exp', split_axis=0, concat_axis=0, tiled=True)  57.8 us
    all_gather x1, waiting for transfers between devices, local(): piece_kv = lax.all_gather(prompt_kv, 'blk', axis=1, tiled=True)  35 us
    unnamed x1, blocking collectives  15.1 us
    all_to_all x1, starting transfers between devices, local(): lax.all_to_all(outgoing, 'exp', split_axis=0, concat_axis=0, tiled=True)  10.2 us
    another operation x4, other arithmetic  9.95 us
    gather x1, local copies, waits for them, and re-layouts, local(): returned.reshape(experts * capacity, D)[slot_index].astype(jnp.float32)  8.11 us
  transfers between devices with their start and end apart: 5, of which 5 were waited for; matrix products, arithmetic and copies ran while one was open for 12% of the time, Pallas kernels for 0%

commit v1 on v0

--- a/solution.py
+++ b/solution.py
@@ -29,6 +29,13 @@
     onehot = (labels[:, None] == jnp.arange(count, dtype=jnp.int32)[None, :]).astype(jnp.int32)
     before = jnp.cumsum(onehot, axis=0) - onehot
     return jnp.sum(before * onehot, axis=1)
+
+
+def gather_rows(piece, axis):
+    count = lax.axis_size(axis)
+    tiles = jnp.broadcast_to(piece[None], (count,) + piece.shape)
+    whole = lax.all_to_all(tiles, axis, split_axis=0, concat_axis=0, tiled=True)
+    return whole.reshape((count * piece.shape[0],) + piece.shape[1:])
 
 
 def absorb(carry_state, query_heads, key_heads, value_heads, visible):
@@ -99,7 +106,7 @@
     attended = (numerator / denom[..., None]).reshape(tok_rows, H * HD).astype(jnp.bfloat16)
     projected = jnp.dot(
         attended,
-        lax.all_gather(out_weight, "exp", axis=0, tiled=True),
+        gather_rows(out_weight, "exp"),
         preferred_element_type=jnp.float32,
     )
     stream = (residual[0].astype(jnp.float32) + projected).astype(jnp.bfloat16)

time: 364 us -> 295 us (0.81)
  waiting for transfers between devices: 244 us -> 150 us
  starting transfers between devices: 22.4 us -> 48.1 us
    all_gather x1 -> x0, waiting for transfers between devices: 84.1 us -> none  [local(): lax.all_gather(out_weight, 'exp', axis=0, tiled=True)]
    all_to_all x1, starting transfers between devices: 4.77 us -> 19.4 us  [local(): lax.all_to_all(dispatch, 'exp', split_axis=0, concat_axis=0, tiled=True)]
    all_to_all x0 -> x1, starting transfers between devices: none -> 14.6 us  [gather_rows(): whole = lax.all_to_all(tiles, axis, split_axis=0, concat_axis=0, tiled=True)]
    all_gather x1, waiting for transfers between devices: 35 us -> 26.5 us  [local(): piece_kv = lax.all_gather(prompt_kv, 'blk', axis=1, tiled=True)]
  transfers between devices with their start and end apart: 5 -> 5, of which waited for: 5 -> 4; matrix products, arithmetic and copies ran while one was open for 12% -> 15% of each run, Pallas kernels for 0% -> 0%
where the time goes in v1:
time: 295 us; the launch traced here: 294 us
  waiting for transfers between devices  150 us (51%)
  starting transfers between devices  48.1 us (16%)
  local copies, waits for them, and re-layouts  32 us (11%)
  other arithmetic  17.4 us (6%)
  matrix products  16.8 us (6%)
  between operations  15.7 us (5%)
  blocking collectives  14 us (5%)
    all_to_all x1, waiting for transfers between devices, local(): lax.all_to_all(outgoing, 'exp', split_axis=0, concat_axis=0, tiled=True)  60 us
    all_to_all x1, waiting for transfers between devices, local(): lax.all_to_all(dispatch, 'exp', split_axis=0, concat_axis=0, tiled=True)  57.8 us
    all_gather x1, waiting for transfers between devices, local(): piece_kv = lax.all_gather(prompt_kv, 'blk', axis=1, tiled=True)  26.5 us
    all_to_all x1, starting transfers between devices, local(): lax.all_to_all(dispatch, 'exp', split_axis=0, concat_axis=0, tiled=True)  19.4 us
    all_to_all x1, starting transfers between devices, gather_rows(): whole = lax.all_to_all(tiles, axis, split_axis=0, concat_axis=0, tiled=True)  14.6 us
    unnamed x1, blocking collectives  14 us
    all_to_all x1, starting transfers between devices, local(): lax.all_to_all(outgoing, 'exp', split_axis=0, concat_axis=0, tiled=True)  10.1 us
    another operation x4, other arithmetic  9.32 us
  transfers between devices with their start and end apart: 5, of which 4 were waited for; matrix products, arithmetic and copies ran while one was open for 15% of the time, Pallas kernels for 0%

profile of v1, /device:TPU:1, one launch (start us, length us, event | category | flops | bytes accessed | tf_op | source)
XLA Modules:
  0.0 294.4 jit_solution(14720587101093367091)
XLA Ops:
  7.2 0.7 all-gather.2.cloned.1.call-update
  7.9 2.4 broadcast_in_dim.94
  10.3 14.6 %all-to-all-start = ((bf16[32,32,1024]{2,1,0:T(8,128)(2,1)}), bf16[32,32,1024]{2,1,0:T(8,128)(2,1)}, u32[]{:S(2)}, u32[]{:S(2)}) async-start(bf16[32,32,1024]{2,1,0:T(8,128)(2,1)} %broadcast_in_dim.94), calls=%async_computation | async-start | bytes 4194304 | tf_op jit(solution)/shard_map/all_to_all | solution.py:37
  26.2 9.0 %reduce-window.19 = s32[32,8,128]{2,1,0:T(8,128)S(1)} reduce-window(s32[32,8,128]{2,1,0:T(8,128)S(1)} %fusion.39, s32[]{:T(128)} %constant.17.clone.1), window={size=1x1x128 pad=0_0x0_0x127_0}, to_apply=%region_6.7 | reduce-window | flops 4161536 | bytes 262148 | tf_op jit(solution)/shard_map/reduce-window.1
  35.6 1.3 dynamic-slice
  38.0 1.1 copy.41
  39.5 14.0 %all-reduce = s32[1024]{0:T(1024)S(1)} all-reduce(s32[1024]{0:T(1024)S(1)} %fusion.43), channel_id=1, replica_groups=mesh['blk'=16,'exp'=32] {'blk'}, use_global_device_ids=true, to_apply=%add | all-reduce | flops 1024 | bytes 8192
  54.9 2.0 select_reduce_fusion
  56.8 26.5 %all-gather.2.cloned.1.call-done = bf16[1,1024,1024]{2,1,0:T(8,128)(2,1)} async-done(((bf16[1,64,1024]{2,1,0:T(8,128)(2,1)}), bf16[1,1024,1024]{2,1,0:T(8,128)(2,1)}) %all-gather.2.cloned.1.call-update) | async-done | bytes 2097168 | tf_op jit(solution)/shard_map/all_gather | solution.py:97
  83.4 2.7 fusion.50
  86.0 1.3 copy.45
  87.4 1.5 copy.44
  88.9 2.9 %fusion = (f32[128,8,2]{0,2,1:T(2,128)S(1)}, f32[8,1024,128,2]{2,1,3,0:T(8,128)S(1)}) fusion(pred[1024]{0:T(1024)(128)(4,1)} %broadcast_compare_fusion, bf16[1024,8,64,1]{0,2,3,1:T(8,128)(2,1)S(1)} %bitcast.130, bf16[128,8,2,64]{0,3,2,1:T(8,128)(2,1)S(1)} %bitcast.133), kind=kOutput, calls=%fused_computation.5 | convolution fusion | flops 274724864 | bytes 9708544 | tf_op jit(solution)/shard_map/tkgd,skd->tkgs/dot_general | solution.py:44
  92.1 2.2 fusion.3
  94.3 1.5 fusion.17
  96.8 2.1 multiply_reduce_fusion
  99.1 7.1 %scatter_custom_fusion = bf16[1280,1024]{1,0:T(8,128)(2,1)} fusion(s32[1024]{0:T(1024)S(1)} %bitcast.144, bf16[]{:T(256)} %constant.12.clone.1, bf16[128,1024]{1,0:T(8,128)(2,1)S(1)} %multiply_convert_fusion), kind=kCustom, calls=%fused_computation.19 | custom fusion | bytes 2883586 | tf_op jit(solution)/shard_map/scatter | solution.py:125
  106.2 19.4 %all-to-all-start.1 = ((bf16[32,40,1024]{2,1,0:T(8,128)(2,1)}), bf16[32,40,1024]{2,1,0:T(8,128)(2,1)}, u32[]{:S(2)}, u32[]{:S(2)}) async-start(bf16[32,40,1024]{2,1,0:T(8,128)(2,1)} %bitcast.129), calls=%async_computation.1 | async-start | bytes 5242880 | tf_op jit(solution)/shard_map/all_to_all | solution.py:128
  125.9 0.9 broadcast_in_dim.98
  126.8 2.1 scatter_fusion
  128.9 57.8 %all-to-all-done.1 = bf16[32,40,1024]{2,1,0:T(8,128)(2,1)} async-done(((bf16[32,40,1024]{2,1,0:T(8,128)(2,1)}), bf16[32,40,1024]{2,1,0:T(8,128)(2,1)}, u32[]{:S(2)}, u32[]{:S(2)}) %all-to-all-start.1) | async-done | bytes 2621472 | tf_op jit(solution)/shard_map/all_to_all | solution.py:128
  186.7 3.9 %all-to-all-start.3 = ((bf16[32,8,1024]{2,1,0:T(8,128)(2,1)}), bf16[32,8,1024]{2,1,0:T(8,128)(2,1)S(1)}, u32[]{:S(2)}, u32[]{:S(2)}) async-start(bf16[32,8,1024]{2,1,0:T(8,128)(2,1)} %scatter_fusion), calls=%async_computation.3 | async-start | bytes 1048576 | tf_op jit(solution)/shard_map/all_to_all | solution.py:159
  190.6 4.7 %fusion.10 = f32[1280,1024]{1,0:T(8,128)S(1)} fusion(bf16[1280,1024]{1,0:T(8,128)(2,1)} %bitcast.33, bf16[1,1024,1024]{2,1,0:T(8,128)(2,1)S(1)} %copy-done), kind=kOutput, calls=%fused_computation.17 | convolution fusion | flops 2684354560 | bytes 9961472 | tf_op jit(solution)/shard_map/dot_general | solution.py:132
  195.4 3.1 %convolution_convert_fusion = bf16[1280,1024]{1,0:T(8,128)(2,1)} fusion(f32[1280,1024]{1,0:T(8,128)S(1)} %fusion.10, bf16[1,512,1024]{2,1,0:T(8,128)(2,1)S(1)} %copy-done.12), kind=kOutput, calls=%fused_computation.14 | convolution fusion | flops 1347420160 | bytes 8912896 | tf_op jit(solution)/shard_map/dot_general | solution.py:134
  198.5 5.3 %all-to-all-done.3 = bf16[32,8,1024]{2,1,0:T(8,128)(2,1)S(1)} async-done(((bf16[32,8,1024]{2,1,0:T(8,128)(2,1)}), bf16[32,8,1024]{2,1,0:T(8,128)(2,1)S(1)}, u32[]{:S(2)}, u32[]{:S(2)}) %all-to-all-start.3) | async-done | bytes 524320 | tf_op jit(solution)/shard_map/all_to_all | solution.py:159
  203.8 10.1 %all-to-all-start.2 = ((bf16[32,40,1024]{2,1,0:T(8,128)(2,1)}), bf16[32,40,1024]{2,1,0:T(8,128)(2,1)}, u32[]{:S(2)}, u32[]{:S(2)}) async-start(bf16[32,40,1024]{2,1,0:T(8,128)(2,1)} %bitcast.131), calls=%async_computation.2 | async-start | bytes 5242880 | tf_op jit(solution)/shard_map/all_to_all | solution.py:139
  214.0 0.9 copy.53
  214.9 60.0 %all-to-all-done.2 = bf16[32,40,1024]{2,1,0:T(8,128)(2,1)} async-done(((bf16[32,40,1024]{2,1,0:T(8,128)(2,1)}), bf16[32,40,1024]{2,1,0:T(8,128)(2,1)}, u32[]{:S(2)}, u32[]{:S(2)}) %all-to-all-start.2) | async-done | bytes 2621472 | tf_op jit(solution)/shard_map/all_to_all | solution.py:139
  274.9 8.1 %gather_fusion = bf16[1024,1024]{1,0:T(8,128)(2,1)} fusion(bf16[1280,1024]{1,0:T(8,128)(2,1)} %bitcast.37, s32[1024]{0:T(1024)S(1)} %broadcast_clamp_fusion), kind=kCustom, calls=%fused_computation | custom fusion | bytes 4198400 | tf_op jit(solution)/shard_map/gather | solution.py:141
  283.0 2.9 fusion.5
  286.0 0.8 fusion.35
  286.7 0.8 copy.66
  (71 shorter events, 4.8 us)
Async XLA Ops:
  7.2 183.4 %copy-start = (bf16[1,1024,1024]{2,1,0:T(8,128)(2,1)S(1)}, bf16[1,1024,1024]{2,1,0:T(8,128)(2,1)}, u32[]{:S(2)}) copy-start(bf16[1,1024,1024]{2,1,0:T(8,128)(2,1)} %param.23) | copy-start | bytes 6291460
  7.2 76.2 %all-gather.2.cloned.1.call-start = ((), (), s32[]{:S(2)}) async-start(), calls=%async_computation.4 | async-start | bytes 2228224 | tf_op jit(solution)/shard_map/all_gather | solution.py:97
  10.3 14.7 %copy-start.13 = (s32[1,2]{1,0:T(1,128)S(1)}, s32[1,2]{1,0:T(1,128)}, u32[]{:S(2)}) copy-start(s32[1,2]{1,0:T(1,128)} %param.18) | copy-start | bytes 28
  10.3 15.5 %copy-start.7 = (s32[1,128,8]{1,2,0:T(8,128)S(1)}, s32[1,128,8]{1,2,0:T(8,128)}, u32[]{:S(2)}) copy-start(s32[1,128,8]{1,2,0:T(8,128)} %param.21) | copy-start | bytes 12292
  10.3 15.7 %copy-start.14 = (s32[1,1,4]{2,1,0:T(1,128)S(1)}, s32[1,1,4]{2,1,0:T(1,128)}, u32[]{:S(2)}) copy-start(s32[1,1,4]{2,1,0:T(1,128)} %param.19) | copy-start | bytes 52
  10.3 27.4 %copy-start.4 = (bf16[1,128,1024]{2,1,0:T(8,128)(2,1)S(1)}, bf16[1,128,1024]{2,1,0:T(8,128)(2,1)}, u32[]{:S(2)}) copy-start(bf16[1,128,1024]{2,1,0:T(8,128)(2,1)} %param.15) | copy-start | bytes 786436
  10.3 85.9 %all-to-all-start = ((bf16[32,32,1024]{2,1,0:T(8,128)(2,1)}), bf16[32,32,1024]{2,1,0:T(8,128)(2,1)}, u32[]{:S(2)}, u32[]{:S(2)}) async-start(bf16[32,32,1024]{2,1,0:T(8,128)(2,1)} %broadcast_in_dim.94), calls=%async_computation | async-start | bytes 4194304 | tf_op jit(solution)/shard_map/all_to_all | solution.py:37
  88.8 3.0 %copy-start.6 = (f32[128,8,2]{0,2,1:T(2,128)S(1)}, f32[128,8,2]{0,2,1:T(2,128)}, u32[]{:S(2)}) copy-start(f32[128,8,2]{0,2,1:T(2,128)} %get-tuple-element.21) | copy-start | bytes 24580
  88.9 3.0 %copy-start.1 = (f32[128,8,2,128]{0,3,2,1:T(8,128)S(1)}, f32[128,8,2,128]{0,3,2,1:T(8,128)}, u32[]{:S(2)}) copy-start(f32[128,8,2,128]{0,3,2,1:T(8,128)} %get-tuple-element.22) | copy-start | bytes 3145732
  88.9 3.2 %copy-start.9 = (pred[1024]{0:T(1024)(128)(4,1)S(1)}, pred[1024]{0:T(1024)(128)(4,1)}, u32[]{:S(2)}) copy-start(pred[1024]{0:T(1024)(128)(4,1)} %broadcast_compare_fusion) | copy-start | bytes 3076
  92.1 2.2 copy-start.2
  95.9 1.0 copy-start.5
  96.2 2.9 copy-start.8
  106.2 19.4 %copy-start.11 = (s32[1,8,1]{1,2,0:T(1,128)S(1)}, s32[1,8,1]{1,2,0:T(1,128)}, u32[]{:S(2)}) copy-start(s32[1,8,1]{1,2,0:T(1,128)} %param.25) | copy-start | bytes 100
  106.2 20.6 %copy-start.3 = (bf16[1,64,1024]{2,1,0:T(8,128)(2,1)S(1)}, bf16[1,64,1024]{2,1,0:T(8,128)(2,1)}, u32[]{:S(2)}) copy-start(bf16[1,64,1024]{2,1,0:T(8,128)(2,1)} %param.16) | copy-start | bytes 393220
  106.2 80.4 %all-to-all-start.1 = ((bf16[32,40,1024]{2,1,0:T(8,128)(2,1)}), bf16[32,40,1024]{2,1,0:T(8,128)(2,1)}, u32[]{:S(2)}, u32[]{:S(2)}) async-start(bf16[32,40,1024]{2,1,0:T(8,128)(2,1)} %bitcast.129), calls=%async_computation.1 | async-start | bytes 5242880 | tf_op jit(solution)/shard_map/all_to_all | solution.py:128
  186.7 17.1 %all-to-all-start.3 = ((bf16[32,8,1024]{2,1,0:T(8,128)(2,1)}), bf16[32,8,1024]{2,1,0:T(8,128)(2,1)S(1)}, u32[]{:S(2)}, u32[]{:S(2)}) async-start(bf16[32,8,1024]{2,1,0:T(8,128)(2,1)} %scatter_fusion), calls=%async_computation.3 | async-start | bytes 1048576 | tf_op jit(solution)/shard_map/all_to_all | solution.py:159
  190.6 4.8 %copy-start.12 = (bf16[1,512,1024]{2,1,0:T(8,128)(2,1)S(1)}, bf16[1,512,1024]{2,1,0:T(8,128)(2,1)}, u32[]{:S(2)}) copy-start(bf16[1,512,1024]{2,1,0:T(8,128)(2,1)} %param.24) | copy-start | bytes 3145732
  203.8 10.1 %copy-start.10 = (f32[1,128,8]{1,2,0:T(8,128)S(1)}, f32[1,128,8]{1,2,0:T(8,128)}, u32[]{:S(2)}) copy-start(f32[1,128,8]{1,2,0:T(8,128)} %param.22) | copy-start | bytes 12292
  203.8 71.1 %all-to-all-start.2 = ((bf16[32,40,1024]{2,1,0:T(8,128)(2,1)}), bf16[32,40,1024]{2,1,0:T(8,128)(2,1)}, u32[]{:S(2)}, u32[]{:S(2)}) async-start(bf16[32,40,1024]{2,1,0:T(8,128)(2,1)} %bitcast.131), calls=%async_computation.2 | async-start | bytes 5242880 | tf_op jit(solution)/shard_map/all_to_all | solution.py:139
Sparse Core Ops, SparseCore 0:
  10.1 73.2 all-gather.1

commit v2 on v1

--- a/solution.py
+++ b/solution.py
@@ -95,7 +95,12 @@
     position_abs = lax.axis_index("blk") * block_rows + jnp.arange(block_rows, dtype=jnp.int32)
     live_keys = ((keep_rows > 0) & (position_abs < prompt_lengths[0])).astype(jnp.int32)[None, :]
     piece_kv = lax.all_gather(prompt_kv, "blk", axis=1, tiled=True)
-    piece_live = lax.all_gather(live_keys, "blk", axis=1, tiled=True)
+    blk_count = lax.axis_size("blk")
+    page_count = block_rows // PAGE
+    packed = jnp.concatenate([live_keys[0], page_owner[0, :, 0]])
+    packed_all = lax.all_gather(packed, "blk", axis=0, tiled=True).reshape(blk_count, -1)
+    piece_live = packed_all[:, :block_rows].reshape(1, -1)
+    owners_all = packed_all[:, block_rows:]
     count = piece_kv.shape[1]
     key_heads = piece_kv[0, :, :kv_width].reshape(count, KVH, HD)
     value_heads = piece_kv[0, :, kv_width:].reshape(count, KVH, HD)
@@ -119,11 +124,11 @@
     capacity = min(tok_rows, 5 * tok_rows * TOPK // (4 * experts))
     flat_routes = routes[0].reshape(-1)
     slot_index = flat_routes * capacity + rank_within(flat_routes, experts)
-    dispatch = (
-        jnp.zeros((experts * capacity, D), jnp.bfloat16)
-        .at[slot_index]
-        .set(jnp.repeat(normed, TOPK, axis=0))
-    )
+    slot_iota = jnp.arange(experts * capacity, dtype=jnp.int32)
+    token_slots = slot_index.reshape(tok_rows, TOPK)
+    hits = token_slots[None, :, :] == slot_iota[:, None, None]
+    placer = jnp.any(hits, axis=-1).astype(jnp.bfloat16)
+    dispatch = jnp.dot(placer, normed, preferred_element_type=jnp.float32).astype(jnp.bfloat16)
     dispatch = dispatch.reshape(experts, capacity, D)
     arrived = lax.all_to_all(dispatch, "exp", split_axis=0, concat_axis=0, tiled=True)
     count = arrived.shape[1]
@@ -137,27 +142,35 @@
     results = [result.reshape(exp_count, count, D)]
     outgoing = jnp.stack(results, axis=1).reshape(exp_count * EXP_DEV, count, D)
     returned = lax.all_to_all(outgoing, "exp", split_axis=0, concat_axis=0, tiled=True)
-    picked = (
-        returned.reshape(experts * capacity, D)[slot_index]
-        .astype(jnp.float32)
-        .reshape(tok_rows, TOPK, D)
+    slot_weight = jnp.sum(
+        jnp.where(
+            token_slots[:, :, None] == slot_iota[None, None, :],
+            route_weight[0][:, :, None],
+            0.0,
+        ),
+        axis=1,
     )
-    layer_out = (stream_f32 + jnp.sum(picked * route_weight[0][:, :, None], axis=1)).astype(
-        jnp.bfloat16
+    combined = jnp.dot(
+        slot_weight,
+        returned.reshape(experts * capacity, D).astype(jnp.float32),
+        precision=lax.Precision.HIGHEST,
+        preferred_element_type=jnp.float32,
     )
-    page_count = block_rows // PAGE
-    blk_count = lax.axis_size("blk")
+    layer_out = (stream_f32 + combined).astype(jnp.bfloat16)
     page_capacity = max(2, 2 * page_count // blk_count)
-    page_rows = prompt_kv[0].reshape(page_count, PAGE, 2 * kv_width)
-    owners = page_owner[0, :, 0]
-    page_slot = owners * page_capacity + rank_within(owners, blk_count)
-    outgoing_pages = (
-        jnp.zeros((blk_count * page_capacity, PAGE, 2 * kv_width), jnp.bfloat16)
-        .at[page_slot]
-        .set(page_rows)
-    )
-    arrived_pages = lax.all_to_all(outgoing_pages, "blk", split_axis=0, concat_axis=0, tiled=True)
-    cache_pages = arrived_pages.reshape(1, blk_count * page_capacity * PAGE, 2 * kv_width)
+    me = lax.axis_index("blk")
+    page_rank = jax.vmap(lambda labels: rank_within(labels, blk_count))(owners_all)
+    block_of = jnp.arange(blk_count, dtype=jnp.int32)[:, None]
+    page_slot = jnp.where(owners_all == me, block_of * page_capacity + page_rank, -1).reshape(-1)
+    out_rows = blk_count * page_capacity * PAGE
+    row_slot = jnp.arange(out_rows, dtype=jnp.int32) // PAGE
+    prompt_rows = piece_kv.shape[1]
+    src_page = jnp.arange(prompt_rows, dtype=jnp.int32) // PAGE
+    same_row = (jnp.arange(out_rows)[:, None] % PAGE) == (jnp.arange(prompt_rows)[None, :] % PAGE)
+    chooser = (page_slot[src_page][None, :] == row_slot[:, None]) & same_row
+    cache_pages = jnp.dot(
+        chooser.astype(jnp.bfloat16), piece_kv[0], preferred_element_type=jnp.float32
+    ).astype(jnp.bfloat16)[None]
     return (attended[None], layer_out[None], cache_pages)
 
 

time: 295 us -> 265 us (0.90)
  blocking collectives: 14 us -> 95.7 us
  waiting for transfers between devices: 150 us -> 69.8 us
  starting transfers between devices: 48.1 us -> 20.7 us
  local copies, waits for them, and re-layouts: 32 us -> 20.7 us
  matrix products: 16.8 us -> 21.3 us
    all_to_all x0 -> x1, blocking collectives: none -> 81 us  [local(): lax.all_to_all(dispatch, 'exp', split_axis=0, concat_axis=0, tiled=True)]
    all_to_all x2 -> x0, waiting for transfers between devices: 63.1 us -> none  [the longest x1 57.8 us: local(): lax.all_to_all(dispatch, 'exp', split_axis=0, concat_axis=0, tiled=True)]
    all_to_all x2 -> x0, starting transfers between devices: 23.3 us -> none  [the longest x1 19.4 us: local(): lax.all_to_all(dispatch, 'exp', split_axis=0, concat_axis=0, tiled=True)]
    all_to_all x1, waiting for transfers between devices: 60 us -> 46.7 us  [local(): lax.all_to_all(outgoing, 'exp', split_axis=0, concat_axis=0, tiled=True)]
    scatter x2 -> x0, local copies, waits for them, and re-layouts: 9.21 us -> none  [the longest x1 7.13 us: local(): dispatch = jnp.zeros((experts * capacity, D), jnp.bfloat16).at[slot_index...]
    dot_general x0 -> x3, matrix products: none -> 7.73 us  [the longest x1 3.69 us: local(): jnp.dot(slot_weight, returned.reshape(experts * capacity, D).astype(jnp.f...]
    reduce_or x0 -> x1, other arithmetic: none -> 5.32 us  [local(): placer = jnp.any(hits, axis=-1).astype(jnp.bfloat16)]
    all_gather x1, waiting for transfers between devices: 26.5 us -> 22.4 us  [local(): piece_kv = lax.all_gather(prompt_kv, 'blk', axis=1, tiled=True)]
  transfers between devices with their start and end apart: 5 -> 3, of which waited for: 4 -> 2; matrix products, arithmetic and copies ran while one was open for 15% -> 18% of each run, Pallas kernels for 0% -> 0%
where the time goes in v2:
time: 265 us; the launch traced here: 264 us
  blocking collectives  95.7 us (36%)
  waiting for transfers between devices  69.8 us (26%)
  matrix products  21.3 us (8%)
  local copies, waits for them, and re-layouts  20.7 us (8%)
  starting transfers between devices  20.7 us (8%)
  other arithmetic  19.9 us (8%)
  between operations  15.8 us (6%)
    all_to_all x1, blocking collectives, local(): lax.all_to_all(dispatch, 'exp', split_axis=0, concat_axis=0, tiled=True)  81 us
    all_to_all x1, waiting for transfers between devices, local(): lax.all_to_all(outgoing, 'exp', split_axis=0, concat_axis=0, tiled=True)  46.7 us
    all_gather x1, waiting for transfers between devices, local(): piece_kv = lax.all_gather(prompt_kv, 'blk', axis=1, tiled=True)  22.4 us
    unnamed x1, blocking collectives  14.7 us
    all_to_all x1, starting transfers between devices, gather_rows(): whole = lax.all_to_all(tiles, axis, split_axis=0, concat_axis=0, tiled=True)  14.6 us
    another operation x4, other arithmetic  9.33 us
    gather x1, local copies, waits for them, and re-layouts, local(): chooser = (page_slot[src_page][None, :] == row_slot[:, None]) & same_row  6.57 us
    all_to_all x1, starting transfers between devices, local(): lax.all_to_all(outgoing, 'exp', split_axis=0, concat_axis=0, tiled=True)  6 us
  transfers between devices with their start and end apart: 3, of which 2 were waited for; matrix products, arithmetic and copies ran while one was open for 18% of the time, Pallas kernels for 0%

profile of v2, /device:TPU:1, one launch (start us, length us, event | category | flops | bytes accessed | tf_op | source)
XLA Modules:
  0.0 263.8 jit_solution(16538950978225094985)
XLA Ops:
  7.2 0.7 all-gather.2.cloned.1.call-update
  7.9 2.4 broadcast_in_dim.111
  10.3 14.6 %all-to-all-start = ((bf16[32,32,1024]{2,1,0:T(8,128)(2,1)}), bf16[32,32,1024]{2,1,0:T(8,128)(2,1)}, u32[]{:S(2)}, u32[]{:S(2)}) async-start(bf16[32,32,1024]{2,1,0:T(8,128)(2,1)} %broadcast_in_dim.111), calls=%async_computation | async-start | bytes 4194304 | tf_op jit(solution)/shard_map/all_to_all | solution.py:37
  26.1 1.3 dynamic-slice
  28.3 14.7 %all-reduce = s32[1152]{0:T(1024)S(1)} all-reduce(s32[1152]{0:T(1024)S(1)} %add_dynamic-update-slice_fusion), channel_id=1, replica_groups=mesh['blk'=16,'exp'=32] {'blk'}, use_global_device_ids=true, to_apply=%add | all-reduce | flops 1152 | bytes 9216
  43.7 0.8 copy.44
  44.4 9.0 %reduce-window.19 = s32[32,8,128]{2,1,0:T(8,128)S(1)} reduce-window(s32[32,8,128]{2,1,0:T(8,128)S(1)} %fusion.52, s32[]{:T(128)} %constant.83.clone.1), window={size=1x1x128 pad=0_0x0_0x127_0}, to_apply=%region_6.7 | reduce-window | flops 4161536 | bytes 262148 | tf_op jit(solution)/shard_map/reduce-window.1
  54.2 5.3 %fusion.5 = pred[1280,128]{1,0:T(8,128)(4,1)} fusion(s32[128,8]{0,1:T(8,128)S(1)} %copy.55), kind=kLoop, calls=%fused_computation.11 | loop fusion | flops 2457600 | bytes 167936 | tf_op jit(solution)/shard_map/reduce_or | solution.py:130
  59.6 1.3 select_reduce_fusion.1
  60.9 22.4 %all-gather.2.cloned.1.call-done = bf16[1,1024,1024]{2,1,0:T(8,128)(2,1)} async-done(((bf16[1,64,1024]{2,1,0:T(8,128)(2,1)}), bf16[1,1024,1024]{2,1,0:T(8,128)(2,1)}) %all-gather.2.cloned.1.call-update) | async-done | bytes 2097168 | tf_op jit(solution)/shard_map/all_gather | solution.py:97
  83.3 2.7 %fusion.65 = (bf16[1,1024,512]{2,1,0:T(8,128)(2,1)}, bf16[1,1024,512]{2,1,0:T(8,128)(2,1)S(1)}) fusion(bf16[1,1024,1024]{2,1,0:T(8,128)(2,1)} %all-gather.2.cloned.1.call-done), kind=kLoop, calls=%fused_computation.108 | loop fusion | bytes 4194304 | tf_op jit(solution)/shard_map/slice | solution.py:105
  86.1 1.3 copy.47
  87.4 1.5 copy.46
  88.9 2.2 fusion
  91.1 0.2 fusion.38
  91.3 2.2 fusion.3
  93.6 1.5 fusion.22
  95.2 0.3 fusion.30
  95.5 0.6 copy-done.7
  96.1 2.1 multiply_reduce_fusion
  98.3 0.9 convolution_convert_fusion.1
  99.2 81.0 %all_to_all.15 = bf16[32,40,1024]{2,1,0:T(8,128)(2,1)S(1)} all-to-all(bf16[32,40,1024]{2,1,0:T(8,128)(2,1)S(1)} %bitcast.124), channel_id=1, replica_groups=mesh['blk'=16,'exp'=32] {'exp'}, dimensions={0} | all-to-all | bytes 5242880 | tf_op jit(solution)/shard_map/all_to_all | solution.py:133
  180.2 2.9 %fusion.12 = f32[1280,1024]{1,0:T(8,128)S(1)} fusion(bf16[1280,1024]{1,0:T(8,128)(2,1)S(1)} %bitcast.127, bf16[1,1024,1024]{2,1,0:T(8,128)(2,1)S(1)} %copy-done), kind=kOutput, calls=%fused_computation.20 | convolution fusion | flops 2684354560 | bytes 9961472 | tf_op jit(solution)/shard_map/dot_general | solution.py:137
  183.1 3.1 %convolution_convert_fusion = bf16[1280,1024]{1,0:T(8,128)(2,1)} fusion(f32[1280,1024]{1,0:T(8,128)S(1)} %fusion.12, bf16[1,512,1024]{2,1,0:T(8,128)(2,1)S(1)} %copy-done.12), kind=kOutput, calls=%fused_computation.14 | convolution fusion | flops 1347420160 | bytes 8912896 | tf_op jit(solution)/shard_map/dot_general | solution.py:139
  186.3 6.0 %all-to-all-start.2 = ((bf16[32,40,1024]{2,1,0:T(8,128)(2,1)}), bf16[32,40,1024]{2,1,0:T(8,128)(2,1)}, u32[]{:S(2)}, u32[]{:S(2)}) async-start(bf16[32,40,1024]{2,1,0:T(8,128)(2,1)} %bitcast.126), calls=%async_computation.2 | async-start | bytes 5242880 | tf_op jit(solution)/shard_map/all_to_all | solution.py:144
  192.7 0.4 select_reduce_fusion.2
  193.3 6.6 %gather_fusion = s32[1024]{0:T(1024)S(1)} fusion(s32[128]{0:T(128)S(1)} %reshape.278, s32[1024]{0:T(1024)S(1)} %broadcast_clamp_fusion), kind=kCustom, calls=%fused_computation | custom fusion | bytes 12288 | tf_op jit(solution)/shard_map/gather | solution.py:170
  199.9 1.6 select_reduce_fusion
  201.6 1.8 copy.56
  203.4 3.1 %fusion.19 = bf16[1,256,1024]{2,1,0:T(8,128)(2,1)} fusion(bf16[1,1024,1024]{2,1,0:T(8,128)(2,1)} %all-gather.2.cloned.1.call-done, s32[1024]{0:T(1024)S(1)} %add_select_fusion.1, s32[1024]{0:T(1024)S(1)} %gather_fusion, s32[256]{0:T(256)S(1)} %get-tuple-element.27, s32[256]{0:T(256)S(1)} %get-tuple-element.28), kind=kOutput, calls=%fused_computation.26 | convolution fusion | flops 537919488 | bytes 2631680 | tf_op jit(solution)/shard_map/dot_general | solution.py:171
  206.5 46.7 %all-to-all-done.2 = bf16[32,40,1024]{2,1,0:T(8,128)(2,1)} async-done(((bf16[32,40,1024]{2,1,0:T(8,128)(2,1)}), bf16[32,40,1024]{2,1,0:T(8,128)(2,1)}, u32[]{:S(2)}, u32[]{:S(2)}) %all-to-all-start.2) | async-done | bytes 2621472 | tf_op jit(solution)/shard_map/all_to_all | solution.py:144
  253.3 3.7 %fusion.33 = bf16[1,128,1024]{2,1,0:T(8,128)(2,1)} fusion(f32[128,1024]{1,0:T(8,128)S(1)} %get-tuple-element.26, f32[128,1280]{1,0:T(8,128)S(1)} %select_reduce_fusion, bf16[1280,1024]{1,0:T(8,128)(2,1)} %bitcast.37), kind=kOutput, calls=%fused_computation.38 | convolution fusion | flops 2013528064 | bytes 4063232 | tf_op jit(solution)/shard_map/dot_general | solution.py:153
  (76 shorter events, 2.9 us)
Async XLA Ops:
  7.2 173.0 %copy-start = (bf16[1,1024,1024]{2,1,0:T(8,128)(2,1)S(1)}, bf16[1,1024,1024]{2,1,0:T(8,128)(2,1)}, u32[]{:S(2)}) copy-start(bf16[1,1024,1024]{2,1,0:T(8,128)(2,1)} %param.23) | copy-start | bytes 6291460
  7.2 76.1 %all-gather.2.cloned.1.call-start = ((), (), s32[]{:S(2)}) async-start(), calls=%async_computation.3 | async-start | bytes 2228224 | tf_op jit(solution)/shard_map/all_gather | solution.py:97
  10.3 14.7 %copy-start.9 = (s32[1,128,8]{1,2,0:T(8,128)S(1)}, s32[1,128,8]{1,2,0:T(8,128)}, u32[]{:S(2)}) copy-start(s32[1,128,8]{1,2,0:T(8,128)} %param.21) | copy-start | bytes 12292
  10.3 15.0 %copy-start.13 = (s32[1,2]{1,0:T(1,128)S(1)}, s32[1,2]{1,0:T(1,128)}, u32[]{:S(2)}) copy-start(s32[1,2]{1,0:T(1,128)} %param.18) | copy-start | bytes 28
  10.3 17.8 %copy-start.11 = (s32[1,8,1]{1,2,0:T(1,128)S(1)}, s32[1,8,1]{1,2,0:T(1,128)}, u32[]{:S(2)}) copy-start(s32[1,8,1]{1,2,0:T(1,128)} %param.25) | copy-start | bytes 100
  10.3 32.8 %copy-start.5 = (bf16[1,128,1024]{2,1,0:T(8,128)(2,1)S(1)}, bf16[1,128,1024]{2,1,0:T(8,128)(2,1)}, u32[]{:S(2)}) copy-start(bf16[1,128,1024]{2,1,0:T(8,128)(2,1)} %param.14) | copy-start | bytes 786436
  10.3 33.0 %copy-start.14 = (s32[1,1,4]{2,1,0:T(1,128)S(1)}, s32[1,1,4]{2,1,0:T(1,128)}, u32[]{:S(2)}) copy-start(s32[1,1,4]{2,1,0:T(1,128)} %param.19) | copy-start | bytes 52
  10.3 33.2 %copy-start.6 = (bf16[1,128,1024]{2,1,0:T(8,128)(2,1)S(1)}, bf16[1,128,1024]{2,1,0:T(8,128)(2,1)}, u32[]{:S(2)}) copy-start(bf16[1,128,1024]{2,1,0:T(8,128)(2,1)} %param.15) | copy-start | bytes 786436
  10.3 85.2 %all-to-all-start = ((bf16[32,32,1024]{2,1,0:T(8,128)(2,1)}), bf16[32,32,1024]{2,1,0:T(8,128)(2,1)}, u32[]{:S(2)}, u32[]{:S(2)}) async-start(bf16[32,32,1024]{2,1,0:T(8,128)(2,1)} %broadcast_in_dim.111), calls=%async_computation | async-start | bytes 4194304 | tf_op jit(solution)/shard_map/all_to_all | solution.py:37
  88.9 2.2 copy-start.1
  91.3 2.3 copy-start.2
  93.6 1.6 copy-start.8
  95.2 1.0 copy-start.7
  95.2 3.1 %copy-start.4 = (pred[1280,128]{1,0:T(8,128)(4,1)S(1)}, pred[1280,128]{1,0:T(8,128)(4,1)}, u32[]{:S(2)}) copy-start(pred[1280,128]{1,0:T(8,128)(4,1)} %fusion.5) | copy-start | bytes 491524
  95.5 3.7 %copy-start.3 = (bf16[128,8,2,64]{0,3,2,1:T(8,128)(2,1)}, bf16[128,8,2,64]{0,3,2,1:T(8,128)(2,1)S(1)}, u32[]{:S(2)}) copy-start(bf16[128,8,2,64]{0,3,2,1:T(8,128)(2,1)S(1)} %fusion.30) | copy-start | bytes 786436
  180.2 2.9 %copy-start.12 = (bf16[1,512,1024]{2,1,0:T(8,128)(2,1)S(1)}, bf16[1,512,1024]{2,1,0:T(8,128)(2,1)}, u32[]{:S(2)}) copy-start(bf16[1,512,1024]{2,1,0:T(8,128)(2,1)} %param.24) | copy-start | bytes 3145732
  186.2 6.2 %copy-start.10 = (f32[1,128,8]{1,2,0:T(8,128)S(1)}, f32[1,128,8]{1,2,0:T(8,128)}, u32[]{:S(2)}) copy-start(f32[1,128,8]{1,2,0:T(8,128)} %param.22) | copy-start | bytes 12292
  186.3 67.0 %all-to-all-start.2 = ((bf16[32,40,1024]{2,1,0:T(8,128)(2,1)}), bf16[32,40,1024]{2,1,0:T(8,128)(2,1)}, u32[]{:S(2)}, u32[]{:S(2)}) async-start(bf16[32,40,1024]{2,1,0:T(8,128)(2,1)} %bitcast.126), calls=%async_computation.2 | async-start | bytes 5242880 | tf_op jit(solution)/shard_map/all_to_all | solution.py:144
Sparse Core Ops, SparseCore 0:
  10.1 73.1 all-gather.1

commit v3 on v2

--- a/solution.py
+++ b/solution.py
@@ -36,6 +36,15 @@
     tiles = jnp.broadcast_to(piece[None], (count,) + piece.shape)
     whole = lax.all_to_all(tiles, axis, split_axis=0, concat_axis=0, tiled=True)
     return whole.reshape((count * piece.shape[0],) + piece.shape[1:])
+
+
+def gather_shifts(piece, axis):
+    count = lax.axis_size(axis)
+    parts = [piece]
+    for shift in range(1, count):
+        pairs = [(j, (j + shift) % count) for j in range(count)]
+        parts.append(lax.ppermute(piece, axis, pairs))
+    return jnp.stack(parts)
 
 
 def absorb(carry_state, query_heads, key_heads, value_heads, visible):
@@ -94,12 +103,15 @@
     keep_rows = jnp.repeat(block_keep[0], KB)
     position_abs = lax.axis_index("blk") * block_rows + jnp.arange(block_rows, dtype=jnp.int32)
     live_keys = ((keep_rows > 0) & (position_abs < prompt_lengths[0])).astype(jnp.int32)[None, :]
-    piece_kv = lax.all_gather(prompt_kv, "blk", axis=1, tiled=True)
     blk_count = lax.axis_size("blk")
+    me = lax.axis_index("blk")
+    piece_kv = gather_shifts(prompt_kv[0], "blk").reshape(1, blk_count * block_rows, -1)
+    source_of = (me - jnp.arange(blk_count, dtype=jnp.int32)) % blk_count
+    global_row = (source_of[:, None] * block_rows + jnp.arange(block_rows, dtype=jnp.int32)).reshape(-1)
     page_count = block_rows // PAGE
     packed = jnp.concatenate([live_keys[0], page_owner[0, :, 0]])
     packed_all = lax.all_gather(packed, "blk", axis=0, tiled=True).reshape(blk_count, -1)
-    piece_live = packed_all[:, :block_rows].reshape(1, -1)
+    piece_live = packed_all[:, :block_rows].reshape(-1)[global_row][None]
     owners_all = packed_all[:, block_rows:]
     count = piece_kv.shape[1]
     key_heads = piece_kv[0, :, :kv_width].reshape(count, KVH, HD)
@@ -158,14 +170,13 @@
     )
     layer_out = (stream_f32 + combined).astype(jnp.bfloat16)
     page_capacity = max(2, 2 * page_count // blk_count)
-    me = lax.axis_index("blk")
     page_rank = jax.vmap(lambda labels: rank_within(labels, blk_count))(owners_all)
     block_of = jnp.arange(blk_count, dtype=jnp.int32)[:, None]
     page_slot = jnp.where(owners_all == me, block_of * page_capacity + page_rank, -1).reshape(-1)
     out_rows = blk_count * page_capacity * PAGE
     row_slot = jnp.arange(out_rows, dtype=jnp.int32) // PAGE
     prompt_rows = piece_kv.shape[1]
-    src_page = jnp.arange(prompt_rows, dtype=jnp.int32) // PAGE
+    src_page = global_row // PAGE
     same_row = (jnp.arange(out_rows)[:, None] % PAGE) == (jnp.arange(prompt_rows)[None, :] % PAGE)
     chooser = (page_slot[src_page][None, :] == row_slot[:, None]) & same_row
     cache_pages = jnp.dot(

time: 265 us -> 300 us (1.13)
  starting transfers between devices: 20.7 us -> 80.3 us
  between operations: 15.8 us -> 2.76 us
  waiting for transfers between devices: 69.8 us -> 58.2 us
  blocking collectives: 95.7 us -> 87.4 us
  local copies, waits for them, and re-layouts: 20.7 us -> 28 us
    ppermute x0 -> x15, starting transfers between devices: none -> 59.5 us  [gather_shifts(): parts.append(lax.ppermute(piece, axis, pairs))]
    all_gather x1 -> x0, waiting for transfers between devices: 22.4 us -> none  [local(): piece_kv = lax.all_gather(prompt_kv, 'blk', axis=1, tiled=True)]
    ppermute x0 -> x15, waiting for transfers between devices: none -> 11.6 us  [gather_shifts(): parts.append(lax.ppermute(piece, axis, pairs))]
    unnamed x35 -> x56, local copies, waits for them, and re-layouts: 3.98 us -> 10.9 us
    all_to_all x1, blocking collectives: 81 us -> 74.1 us  [local(): lax.all_to_all(dispatch, 'exp', split_axis=0, concat_axis=0, tiled=True)]
    gather x0 -> x1, local copies, waits for them, and re-layouts: none -> 4.53 us  [local(): piece_live = packed_all[:, :block_rows].reshape(-1)[global_row][None]]
  transfers between devices with their start and end apart: 3 -> 17, of which waited for: 2 -> 5; matrix products, arithmetic and copies ran while one was open for 18% -> 19% of each run, Pallas kernels for 0% -> 0%
where the time goes in v3:
time: 300 us; the launch traced here: 298 us
  blocking collectives  87.4 us (29%)
  starting transfers between devices  80.3 us (27%)
  waiting for transfers between devices  58.2 us (19%)
  local copies, waits for them, and re-layouts  28 us (9%)
  matrix products  21.3 us (7%)
  other arithmetic  20 us (7%)
    all_to_all x1, blocking collectives, local(): lax.all_to_all(dispatch, 'exp', split_axis=0, concat_axis=0, tiled=True)  74.1 us
    ppermute x15, starting transfers between devices, gather_shifts(): parts.append(lax.ppermute(piece, axis, pairs))  59.5 us
    all_to_all x1, waiting for transfers between devices, local(): lax.all_to_all(outgoing, 'exp', split_axis=0, concat_axis=0, tiled=True)  46.6 us
    all_to_all x1, starting transfers between devices, gather_rows(): whole = lax.all_to_all(tiles, axis, split_axis=0, concat_axis=0, tiled=True)  14.9 us
    unnamed x1, blocking collectives  13.3 us
    ppermute x15, waiting for transfers between devices, gather_shifts(): parts.append(lax.ppermute(piece, axis, pairs))  11.6 us
    unnamed x56, local copies, waits for them, and re-layouts  10.9 us
    another operation x4, other arithmetic  9.33 us
  transfers between devices with their start and end apart: 17, of which 5 were waited for; matrix products, arithmetic and copies ran while one was open for 19% of the time, Pallas kernels for 0%

profile of v3, /device:TPU:1, one launch (start us, length us, event | category | flops | bytes accessed | tf_op | source)
XLA Modules:
  0.0 297.9 jit_solution(6739879867451090384)
XLA Ops:
  0.6 4.2 %collective-permute-start = (bf16[64,1024]{1,0:T(8,128)(2,1)}, bf16[64,1024]{1,0:T(8,128)(2,1)}, u32[]{:S(2)}, u32[]{:S(2)}) collective-permute-start(bf16[64,1024]{1,0:T(8,128)(2,1)} %bitcast.167), channel_id=1, source_target_pairs={{0,32},{32,64},{64,96},{96,128},{128,160},{160,192},{192,224},{224... | collective-permute-start | bytes 393224 | tf_op jit(solution)/shard_map/ppermute | solution.py:46
  4.8 4.2 %collective-permute-start.1 = (bf16[64,1024]{1,0:T(8,128)(2,1)}, bf16[64,1024]{1,0:T(8,128)(2,1)}, u32[]{:S(2)}, u32[]{:S(2)}) collective-permute-start(bf16[64,1024]{1,0:T(8,128)(2,1)} %bitcast.168), channel_id=1, source_target_pairs={{0,64},{32,96},{64,128},{96,160},{128,192},{160,224},{192,256},{22... | collective-permute-start | bytes 393224 | tf_op jit(solution)/shard_map/ppermute | solution.py:46
  9.1 4.6 %collective-permute-start.2 = (bf16[64,1024]{1,0:T(8,128)(2,1)}, bf16[64,1024]{1,0:T(8,128)(2,1)}, u32[]{:S(2)}, u32[]{:S(2)}) collective-permute-start(bf16[64,1024]{1,0:T(8,128)(2,1)} %bitcast.169), channel_id=1, source_target_pairs={{0,96},{32,128},{64,160},{96,192},{128,224},{160,256},{192,288},{2... | collective-permute-start | bytes 393224 | tf_op jit(solution)/shard_map/ppermute | solution.py:46
  13.7 4.5 %collective-permute-start.3 = (bf16[64,1024]{1,0:T(8,128)(2,1)}, bf16[64,1024]{1,0:T(8,128)(2,1)}, u32[]{:S(2)}, u32[]{:S(2)}) collective-permute-start(bf16[64,1024]{1,0:T(8,128)(2,1)} %bitcast.170), channel_id=1, source_target_pairs={{0,128},{32,160},{64,192},{96,224},{128,256},{160,288},{192,320},{... | collective-permute-start | bytes 393224 | tf_op jit(solution)/shard_map/ppermute | solution.py:46
  18.2 4.9 %collective-permute-start.4 = (bf16[64,1024]{1,0:T(8,128)(2,1)}, bf16[64,1024]{1,0:T(8,128)(2,1)S(1)}, u32[]{:S(2)}, u32[]{:S(2)}) collective-permute-start(bf16[64,1024]{1,0:T(8,128)(2,1)} %bitcast.171), channel_id=1, source_target_pairs={{0,160},{32,192},{64,224},{96,256},{128,288},{160,320},{192,352},{... | collective-permute-start | bytes 393224 | tf_op jit(solution)/shard_map/ppermute | solution.py:46
  23.1 2.4 broadcast_in_dim.114
  25.5 14.9 %all-to-all-start = ((bf16[32,32,1024]{2,1,0:T(8,128)(2,1)}), bf16[32,32,1024]{2,1,0:T(8,128)(2,1)}, u32[]{:S(2)}, u32[]{:S(2)}) async-start(bf16[32,32,1024]{2,1,0:T(8,128)(2,1)} %broadcast_in_dim.114), calls=%async_computation | async-start | bytes 4194304 | tf_op jit(solution)/shard_map/all_to_all | solution.py:37
  43.7 13.3 %all-reduce = s32[1152]{0:T(1024)S(1)} all-reduce(s32[1152]{0:T(1024)S(1)} %add_dynamic-update-slice_fusion), channel_id=1, replica_groups=mesh['blk'=16,'exp'=32] {'blk'}, use_global_device_ids=true, to_apply=%add | all-reduce | flops 1152 | bytes 9216
  57.4 4.5 %gather_fusion = s32[1024]{0:T(1024)S(1)} fusion(s32[1024]{0:T(1024)S(1)} %reshape.339, s32[1024]{0:T(1024)S(1)} %broadcast_clamp_fusion.1), kind=kCustom, calls=%fused_computation | custom fusion | bytes 12288 | tf_op jit(solution)/shard_map/gather | solution.py:114
  62.6 9.0 %reduce-window.19 = s32[32,8,128]{2,1,0:T(8,128)S(1)} reduce-window(s32[32,8,128]{2,1,0:T(8,128)S(1)} %fusion.45, s32[]{:T(128)} %constant.95.clone.1), window={size=1x1x128 pad=0_0x0_0x127_0}, to_apply=%region_6.7 | reduce-window | flops 4161536 | bytes 262148 | tf_op jit(solution)/shard_map/reduce-window.1
  73.7 5.3 %fusion.5 = pred[1280,128]{1,0:T(8,128)(4,1)} fusion(s32[128,8]{0,1:T(8,128)S(1)} %copy.55), kind=kLoop, calls=%fused_computation.12 | loop fusion | flops 2457600 | bytes 167936 | tf_op jit(solution)/shard_map/reduce_or | solution.py:142
  82.7 3.1 %collective-permute-start.6 = (bf16[64,1024]{1,0:T(8,128)(2,1)S(1)}, bf16[64,1024]{1,0:T(8,128)(2,1)S(1)}, u32[]{:S(2)}, u32[]{:S(2)}) collective-permute-start(bf16[64,1024]{1,0:T(8,128)(2,1)S(1)} %bitcast.173), channel_id=1, source_target_pairs={{0,224},{32,256},{64,288},{96,320},{128,352},{160,384},{192,416},{... | collective-permute-start | bytes 393224 | tf_op jit(solution)/shard_map/ppermute | solution.py:46
  86.8 2.2 collective-permute-start.7
  89.9 4.1 %collective-permute-start.8 = (bf16[64,1024]{1,0:T(8,128)(2,1)S(1)}, bf16[64,1024]{1,0:T(8,128)(2,1)S(1)}, u32[]{:S(2)}, u32[]{:S(2)}) collective-permute-start(bf16[64,1024]{1,0:T(8,128)(2,1)S(1)} %bitcast.175), channel_id=1, source_target_pairs={{0,288},{32,320},{64,352},{96,384},{128,416},{160,448},{192,480},{... | collective-permute-start | bytes 393224 | tf_op jit(solution)/shard_map/ppermute | solution.py:46
  94.9 4.9 %collective-permute-start.9 = (bf16[64,1024]{1,0:T(8,128)(2,1)S(1)}, bf16[64,1024]{1,0:T(8,128)(2,1)S(1)}, u32[]{:S(2)}, u32[]{:S(2)}) collective-permute-start(bf16[64,1024]{1,0:T(8,128)(2,1)S(1)} %bitcast.176), channel_id=1, source_target_pairs={{0,320},{32,352},{64,384},{96,416},{128,448},{160,480},{192,0},{22... | collective-permute-start | bytes 393224 | tf_op jit(solution)/shard_map/ppermute | solution.py:46
  99.9 5.5 %collective-permute-start.10 = (bf16[64,1024]{1,0:T(8,128)(2,1)S(1)}, bf16[64,1024]{1,0:T(8,128)(2,1)S(1)}, u32[]{:S(2)}, u32[]{:S(2)}) collective-permute-start(bf16[64,1024]{1,0:T(8,128)(2,1)S(1)} %bitcast.177), channel_id=1, source_target_pairs={{0,352},{32,384},{64,416},{96,448},{128,480},{160,0},{192,32},{224... | collective-permute-start | bytes 393224 | tf_op jit(solution)/shard_map/ppermute | solution.py:46
  105.4 2.5 collective-permute-start.11
  108.0 5.5 %collective-permute-start.12 = (bf16[64,1024]{1,0:T(8,128)(2,1)S(1)}, bf16[64,1024]{1,0:T(8,128)(2,1)S(1)}, u32[]{:S(2)}, u32[]{:S(2)}) collective-permute-start(bf16[64,1024]{1,0:T(8,128)(2,1)S(1)} %bitcast.179), channel_id=1, source_target_pairs={{0,416},{32,448},{64,480},{96,0},{128,32},{160,64},{192,96},{224,1... | collective-permute-start | bytes 393224 | tf_op jit(solution)/shard_map/ppermute | solution.py:46
  113.5 4.8 %collective-permute-start.13 = (bf16[64,1024]{1,0:T(8,128)(2,1)S(1)}, bf16[64,1024]{1,0:T(8,128)(2,1)S(1)}, u32[]{:S(2)}, u32[]{:S(2)}) collective-permute-start(bf16[64,1024]{1,0:T(8,128)(2,1)S(1)} %bitcast.180), channel_id=1, source_target_pairs={{0,448},{32,480},{64,0},{96,32},{128,64},{160,96},{192,128},{224,1... | collective-permute-start | bytes 393224 | tf_op jit(solution)/shard_map/ppermute | solution.py:46
  118.4 2.5 collective-permute-start.14
  121.5 2.7 collective-permute-done.12
  124.2 7.2 %collective-permute-done.13 = bf16[64,1024]{1,0:T(8,128)(2,1)S(1)} collective-permute-done((bf16[64,1024]{1,0:T(8,128)(2,1)S(1)}, bf16[64,1024]{1,0:T(8,128)(2,1)S(1)}, u32[]{:S(2)}, u32[]{:S(2)}) %collective-permute-start.13) | collective-permute-done | bytes 131104 | tf_op jit(solution)/shard_map/ppermute | solution.py:46
  137.1 2.2 fusion
  139.6 2.2 fusion.3
  147.4 74.1 %all_to_all.15 = bf16[32,40,1024]{2,1,0:T(8,128)(2,1)S(1)} all-to-all(bf16[32,40,1024]{2,1,0:T(8,128)(2,1)S(1)} %bitcast.153), channel_id=1, replica_groups=mesh['blk'=16,'exp'=32] {'exp'}, dimensions={0} | all-to-all | bytes 5242880 | tf_op jit(solution)/shard_map/all_to_all | solution.py:145
  221.5 2.9 fusion.10
  224.5 3.1 %convolution_convert_fusion = bf16[1280,1024]{1,0:T(8,128)(2,1)} fusion(f32[1280,1024]{1,0:T(8,128)S(1)} %fusion.10, bf16[1,512,1024]{2,1,0:T(8,128)(2,1)S(1)} %copy-done.14), kind=kOutput, calls=%fused_computation.15 | convolution fusion | flops 1347420160 | bytes 8912896 | tf_op jit(solution)/shard_map/dot_general | solution.py:151
  227.6 5.8 %all-to-all-start.2 = ((bf16[32,40,1024]{2,1,0:T(8,128)(2,1)}), bf16[32,40,1024]{2,1,0:T(8,128)(2,1)}, u32[]{:S(2)}, u32[]{:S(2)}) async-start(bf16[32,40,1024]{2,1,0:T(8,128)(2,1)} %bitcast.155), calls=%async_computation.2 | async-start | bytes 5242880 | tf_op jit(solution)/shard_map/all_to_all | solution.py:156
  234.5 6.6 %gather_fusion.1 = s32[1024]{0:T(1024)S(1)} fusion(s32[128]{0:T(128)S(1)} %reshape.345, s32[1024]{0:T(1024)S(1)} %broadcast_clamp_fusion), kind=kCustom, calls=%fused_computation.1 | custom fusion | bytes 12288 | tf_op jit(solution)/shard_map/gather | solution.py:181
  244.5 3.1 %fusion.14 = bf16[1,256,1024]{2,1,0:T(8,128)(2,1)} fusion(bf16[1024,1024]{1,0:T(8,128)(2,1)} %bitcast.158, s32[1024]{0:T(1024)S(1)} %add_select_fusion.1, s32[1024]{0:T(1024)S(1)} %gather_fusion.1, s32[256]{0:T(256)S(1)} %get-tuple-element.29, s32[256]{0:T(256)S(1)} %get-tuple-element.30), kind=kOutput, calls=%fused_computation.25 | convolution fusion | flops 537919488 | bytes 2631680 | tf_op jit(solution)/shard_map/dot_general | solution.py:182
  247.7 46.6 %all-to-all-done.2 = bf16[32,40,1024]{2,1,0:T(8,128)(2,1)} async-done(((bf16[32,40,1024]{2,1,0:T(8,128)(2,1)}), bf16[32,40,1024]{2,1,0:T(8,128)(2,1)}, u32[]{:S(2)}, u32[]{:S(2)}) %all-to-all-start.2) | async-done | bytes 2621472 | tf_op jit(solution)/shard_map/all_to_all | solution.py:156
  294.2 3.7 %fusion.26 = bf16[1,128,1024]{2,1,0:T(8,128)(2,1)} fusion(f32[128,1024]{1,0:T(8,128)S(1)} %get-tuple-element.28, f32[128,1280]{1,0:T(8,128)S(1)} %select_reduce_fusion, bf16[1280,1024]{1,0:T(8,128)(2,1)} %bitcast.55), kind=kOutput, calls=%fused_computation.37 | convolution fusion | flops 2013528064 | bytes 4063232 | tf_op jit(solution)/shard_map/dot_general | solution.py:165
  (128 shorter events, 27.9 us)
Async XLA Ops:
  0.6 220.9 %copy-start = (bf16[1,1024,1024]{2,1,0:T(8,128)(2,1)S(1)}, bf16[1,1024,1024]{2,1,0:T(8,128)(2,1)}, u32[]{:S(2)}) copy-start(bf16[1,1024,1024]{2,1,0:T(8,128)(2,1)} %param.23) | copy-start | bytes 6291460
  0.6 79.1 %collective-permute-start = (bf16[64,1024]{1,0:T(8,128)(2,1)}, bf16[64,1024]{1,0:T(8,128)(2,1)}, u32[]{:S(2)}, u32[]{:S(2)}) collective-permute-start(bf16[64,1024]{1,0:T(8,128)(2,1)} %bitcast.167), channel_id=1, source_target_pairs={{0,32},{32,64},{64,96},{96,128},{128,160},{160,192},{192,224},{224... | collective-permute-start | bytes 393224 | tf_op jit(solution)/shard_map/ppermute | solution.py:46
  4.8 77.9 %collective-permute-start.1 = (bf16[64,1024]{1,0:T(8,128)(2,1)}, bf16[64,1024]{1,0:T(8,128)(2,1)}, u32[]{:S(2)}, u32[]{:S(2)}) collective-permute-start(bf16[64,1024]{1,0:T(8,128)(2,1)} %bitcast.168), channel_id=1, source_target_pairs={{0,64},{32,96},{64,128},{96,160},{128,192},{160,224},{192,256},{22... | collective-permute-start | bytes 393224 | tf_op jit(solution)/shard_map/ppermute | solution.py:46
  9.1 77.7 %collective-permute-start.2 = (bf16[64,1024]{1,0:T(8,128)(2,1)}, bf16[64,1024]{1,0:T(8,128)(2,1)}, u32[]{:S(2)}, u32[]{:S(2)}) collective-permute-start(bf16[64,1024]{1,0:T(8,128)(2,1)} %bitcast.169), channel_id=1, source_target_pairs={{0,96},{32,128},{64,160},{96,192},{128,224},{160,256},{192,288},{2... | collective-permute-start | bytes 393224 | tf_op jit(solution)/shard_map/ppermute | solution.py:46
  13.7 76.2 %collective-permute-start.3 = (bf16[64,1024]{1,0:T(8,128)(2,1)}, bf16[64,1024]{1,0:T(8,128)(2,1)}, u32[]{:S(2)}, u32[]{:S(2)}) collective-permute-start(bf16[64,1024]{1,0:T(8,128)(2,1)} %bitcast.170), channel_id=1, source_target_pairs={{0,128},{32,160},{64,192},{96,224},{128,256},{160,288},{192,320},{... | collective-permute-start | bytes 393224 | tf_op jit(solution)/shard_map/ppermute | solution.py:46
  18.2 76.7 %collective-permute-start.4 = (bf16[64,1024]{1,0:T(8,128)(2,1)}, bf16[64,1024]{1,0:T(8,128)(2,1)S(1)}, u32[]{:S(2)}, u32[]{:S(2)}) collective-permute-start(bf16[64,1024]{1,0:T(8,128)(2,1)} %bitcast.171), channel_id=1, source_target_pairs={{0,160},{32,192},{64,224},{96,256},{128,288},{160,320},{192,352},{... | collective-permute-start | bytes 393224 | tf_op jit(solution)/shard_map/ppermute | solution.py:46
  25.5 14.9 %copy-start.11 = (s32[1,128,8]{1,2,0:T(8,128)S(1)}, s32[1,128,8]{1,2,0:T(8,128)}, u32[]{:S(2)}) copy-start(s32[1,128,8]{1,2,0:T(8,128)} %param.21) | copy-start | bytes 12292
  25.5 15.2 %copy-start.15 = (s32[1,2]{1,0:T(1,128)S(1)}, s32[1,2]{1,0:T(1,128)}, u32[]{:S(2)}) copy-start(s32[1,2]{1,0:T(1,128)} %param.18) | copy-start | bytes 28
  25.5 18.0 %copy-start.13 = (s32[1,8,1]{1,2,0:T(1,128)S(1)}, s32[1,8,1]{1,2,0:T(1,128)}, u32[]{:S(2)}) copy-start(s32[1,8,1]{1,2,0:T(1,128)} %param.25) | copy-start | bytes 100
  25.5 118.3 %all-to-all-start = ((bf16[32,32,1024]{2,1,0:T(8,128)(2,1)}), bf16[32,32,1024]{2,1,0:T(8,128)(2,1)}, u32[]{:S(2)}, u32[]{:S(2)}) async-start(bf16[32,32,1024]{2,1,0:T(8,128)(2,1)} %broadcast_in_dim.114), calls=%async_computation | async-start | bytes 4194304 | tf_op jit(solution)/shard_map/all_to_all | solution.py:37
  57.3 4.6 %copy-start.6 = (bf16[1,128,1024]{2,1,0:T(8,128)(2,1)S(1)}, bf16[1,128,1024]{2,1,0:T(8,128)(2,1)}, u32[]{:S(2)}) copy-start(bf16[1,128,1024]{2,1,0:T(8,128)(2,1)} %param.14) | copy-start | bytes 786436
  57.3 4.8 %copy-start.16 = (s32[1,1,4]{2,1,0:T(1,128)S(1)}, s32[1,1,4]{2,1,0:T(1,128)}, u32[]{:S(2)}) copy-start(s32[1,1,4]{2,1,0:T(1,128)} %param.19) | copy-start | bytes 52
  57.3 5.1 %copy-start.7 = (bf16[1,128,1024]{2,1,0:T(8,128)(2,1)S(1)}, bf16[1,128,1024]{2,1,0:T(8,128)(2,1)}, u32[]{:S(2)}) copy-start(bf16[1,128,1024]{2,1,0:T(8,128)(2,1)} %param.15) | copy-start | bytes 786436
  62.5 17.3 %copy-start.9 = (bf16[1,64,1024]{2,1,0:T(8,128)(2,1)S(1)}, bf16[1,64,1024]{2,1,0:T(8,128)(2,1)}, u32[]{:S(2)}) copy-start(bf16[1,64,1024]{2,1,0:T(8,128)(2,1)} %param.16) | copy-start | bytes 393220
  79.8 20.1 %collective-permute-start.5 = (bf16[64,1024]{1,0:T(8,128)(2,1)S(1)}, bf16[64,1024]{1,0:T(8,128)(2,1)S(1)}, u32[]{:S(2)}, u32[]{:S(2)}) collective-permute-start(bf16[64,1024]{1,0:T(8,128)(2,1)S(1)} %bitcast.172), channel_id=1, source_target_pairs={{0,192},{32,224},{64,256},{96,288},{128,320},{160,352},{192,384},{... | collective-permute-start | bytes 393224 | tf_op jit(solution)/shard_map/ppermute | solution.py:46
  82.7 22.7 %collective-permute-start.6 = (bf16[64,1024]{1,0:T(8,128)(2,1)S(1)}, bf16[64,1024]{1,0:T(8,128)(2,1)S(1)}, u32[]{:S(2)}, u32[]{:S(2)}) collective-permute-start(bf16[64,1024]{1,0:T(8,128)(2,1)S(1)} %bitcast.173), channel_id=1, source_target_pairs={{0,224},{32,256},{64,288},{96,320},{128,352},{160,384},{192,416},{... | collective-permute-start | bytes 393224 | tf_op jit(solution)/shard_map/ppermute | solution.py:46
  86.8 21.2 %collective-permute-start.7 = (bf16[64,1024]{1,0:T(8,128)(2,1)S(1)}, bf16[64,1024]{1,0:T(8,128)(2,1)S(1)}, u32[]{:S(2)}, u32[]{:S(2)}) collective-permute-start(bf16[64,1024]{1,0:T(8,128)(2,1)S(1)} %bitcast.174), channel_id=1, source_target_pairs={{0,256},{32,288},{64,320},{96,352},{128,384},{160,416},{192,448},{... | collective-permute-start | bytes 393224 | tf_op jit(solution)/shard_map/ppermute | solution.py:46
  89.9 23.6 %collective-permute-start.8 = (bf16[64,1024]{1,0:T(8,128)(2,1)S(1)}, bf16[64,1024]{1,0:T(8,128)(2,1)S(1)}, u32[]{:S(2)}, u32[]{:S(2)}) collective-permute-start(bf16[64,1024]{1,0:T(8,128)(2,1)S(1)} %bitcast.175), channel_id=1, source_target_pairs={{0,288},{32,320},{64,352},{96,384},{128,416},{160,448},{192,480},{... | collective-permute-start | bytes 393224 | tf_op jit(solution)/shard_map/ppermute | solution.py:46
  94.9 23.4 %collective-permute-start.9 = (bf16[64,1024]{1,0:T(8,128)(2,1)S(1)}, bf16[64,1024]{1,0:T(8,128)(2,1)S(1)}, u32[]{:S(2)}, u32[]{:S(2)}) collective-permute-start(bf16[64,1024]{1,0:T(8,128)(2,1)S(1)} %bitcast.176), channel_id=1, source_target_pairs={{0,320},{32,352},{64,384},{96,416},{128,448},{160,480},{192,0},{22... | collective-permute-start | bytes 393224 | tf_op jit(solution)/shard_map/ppermute | solution.py:46
  99.9 21.0 %collective-permute-start.10 = (bf16[64,1024]{1,0:T(8,128)(2,1)S(1)}, bf16[64,1024]{1,0:T(8,128)(2,1)S(1)}, u32[]{:S(2)}, u32[]{:S(2)}) collective-permute-start(bf16[64,1024]{1,0:T(8,128)(2,1)S(1)} %bitcast.177), channel_id=1, source_target_pairs={{0,352},{32,384},{64,416},{96,448},{128,480},{160,0},{192,32},{224... | collective-permute-start | bytes 393224 | tf_op jit(solution)/shard_map/ppermute | solution.py:46
  105.4 16.0 %collective-permute-start.11 = (bf16[64,1024]{1,0:T(8,128)(2,1)S(1)}, bf16[64,1024]{1,0:T(8,128)(2,1)S(1)}, u32[]{:S(2)}, u32[]{:S(2)}) collective-permute-start(bf16[64,1024]{1,0:T(8,128)(2,1)S(1)} %bitcast.178), channel_id=1, source_target_pairs={{0,384},{32,416},{64,448},{96,480},{128,0},{160,32},{192,64},{224,... | collective-permute-start | bytes 393224 | tf_op jit(solution)/shard_map/ppermute | solution.py:46
  108.0 16.2 %collective-permute-start.12 = (bf16[64,1024]{1,0:T(8,128)(2,1)S(1)}, bf16[64,1024]{1,0:T(8,128)(2,1)S(1)}, u32[]{:S(2)}, u32[]{:S(2)}) collective-permute-start(bf16[64,1024]{1,0:T(8,128)(2,1)S(1)} %bitcast.179), channel_id=1, source_target_pairs={{0,416},{32,448},{64,480},{96,0},{128,32},{160,64},{192,96},{224,1... | collective-permute-start | bytes 393224 | tf_op jit(solution)/shard_map/ppermute | solution.py:46
  113.5 17.9 %collective-permute-start.13 = (bf16[64,1024]{1,0:T(8,128)(2,1)S(1)}, bf16[64,1024]{1,0:T(8,128)(2,1)S(1)}, u32[]{:S(2)}, u32[]{:S(2)}) collective-permute-start(bf16[64,1024]{1,0:T(8,128)(2,1)S(1)} %bitcast.180), channel_id=1, source_target_pairs={{0,448},{32,480},{64,0},{96,32},{128,64},{160,96},{192,128},{224,1... | collective-permute-start | bytes 393224 | tf_op jit(solution)/shard_map/ppermute | solution.py:46
  118.4 14.2 %collective-permute-start.14 = (bf16[64,1024]{1,0:T(8,128)(2,1)S(1)}, bf16[64,1024]{1,0:T(8,128)(2,1)S(1)}, u32[]{:S(2)}, u32[]{:S(2)}) collective-permute-start(bf16[64,1024]{1,0:T(8,128)(2,1)S(1)} %bitcast.181), channel_id=1, source_target_pairs={{0,480},{32,0},{64,32},{96,64},{128,96},{160,128},{192,160},{224,1... | collective-permute-start | bytes 393224 | tf_op jit(solution)/shard_map/ppermute | solution.py:46
  132.6 1.7 copy-start.2
  137.1 2.3 copy-start.1
  139.6 2.3 copy-start.3
  143.7 3.7 %copy-start.4 = (bf16[128,8,2,64]{0,3,2,1:T(8,128)(2,1)}, bf16[128,8,2,64]{0,3,2,1:T(8,128)(2,1)S(1)}, u32[]{:S(2)}) copy-start(bf16[128,8,2,64]{0,3,2,1:T(8,128)(2,1)S(1)} %fusion.23) | copy-start | bytes 786436
  143.8 2.7 copy-start.5
  221.5 2.9 copy-start.14
  227.6 6.0 %copy-start.12 = (f32[1,128,8]{1,2,0:T(8,128)S(1)}, f32[1,128,8]{1,2,0:T(8,128)}, u32[]{:S(2)}) copy-start(f32[1,128,8]{1,2,0:T(8,128)} %param.22) | copy-start | bytes 12292
  227.6 66.6 %all-to-all-start.2 = ((bf16[32,40,1024]{2,1,0:T(8,128)(2,1)}), bf16[32,40,1024]{2,1,0:T(8,128)(2,1)}, u32[]{:S(2)}, u32[]{:S(2)}) async-start(bf16[32,40,1024]{2,1,0:T(8,128)(2,1)} %bitcast.155), calls=%async_computation.2 | async-start | bytes 5242880 | tf_op jit(solution)/shard_map/all_to_all | solution.py:156
  (2 other events, 2.5 us)

commit v4 on v2

--- a/solution.py
+++ b/solution.py
@@ -94,7 +94,7 @@
     keep_rows = jnp.repeat(block_keep[0], KB)
     position_abs = lax.axis_index("blk") * block_rows + jnp.arange(block_rows, dtype=jnp.int32)
     live_keys = ((keep_rows > 0) & (position_abs < prompt_lengths[0])).astype(jnp.int32)[None, :]
-    piece_kv = lax.all_gather(prompt_kv, "blk", axis=1, tiled=True)
+    piece_kv = gather_rows(prompt_kv[0], "blk")[None]
     blk_count = lax.axis_size("blk")
     page_count = block_rows // PAGE
     packed = jnp.concatenate([live_keys[0], page_owner[0, :, 0]])
@@ -111,7 +111,7 @@
     attended = (numerator / denom[..., None]).reshape(tok_rows, H * HD).astype(jnp.bfloat16)
     projected = jnp.dot(
         attended,
-        gather_rows(out_weight, "exp"),
+        lax.all_gather(out_weight, "exp", axis=0, tiled=True),
         preferred_element_type=jnp.float32,
     )
     stream = (residual[0].astype(jnp.float32) + projected).astype(jnp.bfloat16)

time: 265 us -> 272 us (1.026)
  blocking collectives: 95.7 us -> 121 us
  waiting for transfers between devices: 69.8 us -> 57.3 us
  starting transfers between devices: 20.7 us -> 14.9 us
    unnamed x1, blocking collectives: 14.7 us -> 53 us
    all_to_all x1, blocking collectives: 81 us -> 68.1 us  [local(): lax.all_to_all(dispatch, 'exp', split_axis=0, concat_axis=0, tiled=True)]
    all_gather x1, waiting for transfers between devices: 22.4 us -> 9.88 us  [local(): lax.all_gather(out_weight, 'exp', axis=0, tiled=True)]
    all_to_all x1, starting transfers between devices: 14.6 us -> 8.88 us  [gather_rows(): whole = lax.all_to_all(tiles, axis, split_axis=0, concat_axis=0, tiled=True)]
  transfers between devices with their start and end apart: 3 -> 3, of which waited for: 2 -> 2; matrix products, arithmetic and copies ran while one was open for 18% -> 17% of each run, Pallas kernels for 0% -> 0%
where the time goes in v4:
time: 272 us; the launch traced here: 271 us
  blocking collectives  121 us (44%)
  waiting for transfers between devices  57.3 us (21%)
  matrix products  21.3 us (8%)
  local copies, waits for them, and re-layouts  20.2 us (7%)
  other arithmetic  19.9 us (7%)
  between operations  15.8 us (6%)
  starting transfers between devices  14.9 us (5%)
    all_to_all x1, blocking collectives, local(): lax.all_to_all(dispatch, 'exp', split_axis=0, concat_axis=0, tiled=True)  68.1 us
    unnamed x1, blocking collectives  53 us
    all_to_all x1, waiting for transfers between devices, local(): lax.all_to_all(outgoing, 'exp', split_axis=0, concat_axis=0, tiled=True)  46.8 us
    all_gather x1, waiting for transfers between devices, local(): lax.all_gather(out_weight, 'exp', axis=0, tiled=True)  9.88 us
    another operation x4, other arithmetic  9.33 us
    all_to_all x1, starting transfers between devices, gather_rows(): whole = lax.all_to_all(tiles, axis, split_axis=0, concat_axis=0, tiled=True)  8.88 us
    gather x1, local copies, waits for them, and re-layouts, local(): chooser = (page_slot[src_page][None, :] == row_slot[:, None]) & same_row  6.57 us
    all_to_all x1, starting transfers between devices, local(): lax.all_to_all(outgoing, 'exp', split_axis=0, concat_axis=0, tiled=True)  6.01 us
  transfers between devices with their start and end apart: 3, of which 2 were waited for; matrix products, arithmetic and copies ran while one was open for 17% of the time, Pallas kernels for 0%

profile of v4, /device:TPU:1, one launch (start us, length us, event | category | flops | bytes accessed | tf_op | source)
XLA Modules:
  0.0 270.6 jit_solution(15563441076086219965)
XLA Ops:
  7.2 2.6 broadcast_in_dim.111
  9.8 8.9 %all-to-all-start = ((bf16[16,64,1024]{2,1,0:T(8,128)(2,1)}), bf16[16,64,1024]{2,1,0:T(8,128)(2,1)}, u32[]{:S(2)}, u32[]{:S(2)}) async-start(bf16[16,64,1024]{2,1,0:T(8,128)(2,1)} %broadcast_in_dim.111), calls=%async_computation | async-start | bytes 4194304 | tf_op jit(solution)/shard_map/all_to_all | solution.py:37
  18.8 0.7 all-gather.2.cloned.1.call-update
  20.6 1.3 dynamic-slice
  22.6 0.2 add_dynamic-update-slice_fusion
  22.7 53.0 %all-reduce = s32[1152]{0:T(1024)S(1)} all-reduce(s32[1152]{0:T(1024)S(1)} %add_dynamic-update-slice_fusion), channel_id=1, replica_groups=mesh['blk'=16,'exp'=32] {'blk'}, use_global_device_ids=true, to_apply=%add | all-reduce | flops 1152 | bytes 9216
  76.5 0.8 copy.43
  77.3 9.0 %reduce-window.19 = s32[32,8,128]{2,1,0:T(8,128)S(1)} reduce-window(s32[32,8,128]{2,1,0:T(8,128)S(1)} %fusion.45, s32[]{:T(128)} %constant.83.clone.1), window={size=1x1x128 pad=0_0x0_0x127_0}, to_apply=%region_6.7 | reduce-window | flops 4161536 | bytes 262148 | tf_op jit(solution)/shard_map/reduce-window.1
  87.0 5.3 %fusion.5 = pred[1280,128]{1,0:T(8,128)(4,1)} fusion(s32[128,8]{0,1:T(8,128)S(1)} %copy.54), kind=kLoop, calls=%fused_computation.11 | loop fusion | flops 2457600 | bytes 167936 | tf_op jit(solution)/shard_map/reduce_or | solution.py:130
  92.4 1.3 select_reduce_fusion.1
  93.8 2.7 fusion.58
  96.4 1.3 copy.46
  97.8 1.5 copy.45
  99.3 2.2 fusion
  101.5 0.2 fusion.31
  101.7 2.2 fusion.3
  104.0 1.5 fusion.15
  105.6 0.3 fusion.23
  105.9 9.9 %all-gather.2.cloned.1.call-done = bf16[1024,1024]{1,0:T(8,128)(2,1)} async-done(((bf16[32,1024]{1,0:T(8,128)(2,1)}), bf16[1024,1024]{1,0:T(8,128)(2,1)}) %all-gather.2.cloned.1.call-update) | async-done | bytes 2097168 | tf_op jit(solution)/shard_map/all_gather | solution.py:114
  115.8 2.1 multiply_reduce_fusion
  118.0 0.9 convolution_convert_fusion.1
  118.9 68.1 %all_to_all.15 = bf16[32,40,1024]{2,1,0:T(8,128)(2,1)S(1)} all-to-all(bf16[32,40,1024]{2,1,0:T(8,128)(2,1)S(1)} %bitcast.120), channel_id=1, replica_groups=mesh['blk'=16,'exp'=32] {'exp'}, dimensions={0} | all-to-all | bytes 5242880 | tf_op jit(solution)/shard_map/all_to_all | solution.py:133
  187.0 2.9 %fusion.10 = f32[1280,1024]{1,0:T(8,128)S(1)} fusion(bf16[1280,1024]{1,0:T(8,128)(2,1)S(1)} %bitcast.123, bf16[1,1024,1024]{2,1,0:T(8,128)(2,1)S(1)} %copy-done), kind=kOutput, calls=%fused_computation.18 | convolution fusion | flops 2684354560 | bytes 9961472 | tf_op jit(solution)/shard_map/dot_general | solution.py:137
  189.9 3.1 %convolution_convert_fusion = bf16[1280,1024]{1,0:T(8,128)(2,1)} fusion(f32[1280,1024]{1,0:T(8,128)S(1)} %fusion.10, bf16[1,512,1024]{2,1,0:T(8,128)(2,1)S(1)} %copy-done.12), kind=kOutput, calls=%fused_computation.14 | convolution fusion | flops 1347420160 | bytes 8912896 | tf_op jit(solution)/shard_map/dot_general | solution.py:139
  193.0 6.0 %all-to-all-start.2 = ((bf16[32,40,1024]{2,1,0:T(8,128)(2,1)}), bf16[32,40,1024]{2,1,0:T(8,128)(2,1)}, u32[]{:S(2)}, u32[]{:S(2)}) async-start(bf16[32,40,1024]{2,1,0:T(8,128)(2,1)} %bitcast.122), calls=%async_computation.2 | async-start | bytes 5242880 | tf_op jit(solution)/shard_map/all_to_all | solution.py:144
  199.5 0.4 select_reduce_fusion.2
  200.1 6.6 %gather_fusion = s32[1024]{0:T(1024)S(1)} fusion(s32[128]{0:T(128)S(1)} %reshape.273, s32[1024]{0:T(1024)S(1)} %broadcast_clamp_fusion), kind=kCustom, calls=%fused_computation | custom fusion | bytes 12288 | tf_op jit(solution)/shard_map/gather | solution.py:170
  206.7 1.6 select_reduce_fusion
  208.4 1.8 copy.55
  210.2 3.1 %fusion.14 = bf16[1,256,1024]{2,1,0:T(8,128)(2,1)} fusion(bf16[1024,1024]{1,0:T(8,128)(2,1)} %bitcast.41, s32[1024]{0:T(1024)S(1)} %add_select_fusion.1, s32[1024]{0:T(1024)S(1)} %gather_fusion, s32[256]{0:T(256)S(1)} %get-tuple-element.27, s32[256]{0:T(256)S(1)} %get-tuple-element.28), kind=kOutput, calls=%fused_computation.24 | convolution fusion | flops 537919488 | bytes 2631680 | tf_op jit(solution)/shard_map/dot_general | solution.py:171
  213.3 46.8 %all-to-all-done.2 = bf16[32,40,1024]{2,1,0:T(8,128)(2,1)} async-done(((bf16[32,40,1024]{2,1,0:T(8,128)(2,1)}), bf16[32,40,1024]{2,1,0:T(8,128)(2,1)}, u32[]{:S(2)}, u32[]{:S(2)}) %all-to-all-start.2) | async-done | bytes 2621472 | tf_op jit(solution)/shard_map/all_to_all | solution.py:144
  260.0 3.7 %fusion.26 = bf16[1,128,1024]{2,1,0:T(8,128)(2,1)} fusion(f32[128,1024]{1,0:T(8,128)S(1)} %get-tuple-element.26, f32[128,1280]{1,0:T(8,128)S(1)} %select_reduce_fusion, bf16[1280,1024]{1,0:T(8,128)(2,1)} %bitcast.38), kind=kOutput, calls=%fused_computation.36 | convolution fusion | flops 2013528064 | bytes 4063232 | tf_op jit(solution)/shard_map/dot_general | solution.py:153
  (76 shorter events, 2.7 us)
Async XLA Ops:
  7.2 179.8 %copy-start = (bf16[1,1024,1024]{2,1,0:T(8,128)(2,1)S(1)}, bf16[1,1024,1024]{2,1,0:T(8,128)(2,1)}, u32[]{:S(2)}) copy-start(bf16[1,1024,1024]{2,1,0:T(8,128)(2,1)} %param.23) | copy-start | bytes 6291460
  9.8 9.7 %copy-start.9 = (s32[1,128,8]{1,2,0:T(8,128)S(1)}, s32[1,128,8]{1,2,0:T(8,128)}, u32[]{:S(2)}) copy-start(s32[1,128,8]{1,2,0:T(8,128)} %param.21) | copy-start | bytes 12292
  9.8 10.0 %copy-start.13 = (s32[1,2]{1,0:T(1,128)S(1)}, s32[1,2]{1,0:T(1,128)}, u32[]{:S(2)}) copy-start(s32[1,2]{1,0:T(1,128)} %param.18) | copy-start | bytes 28
  9.8 12.8 %copy-start.11 = (s32[1,8,1]{1,2,0:T(1,128)S(1)}, s32[1,8,1]{1,2,0:T(1,128)}, u32[]{:S(2)}) copy-start(s32[1,8,1]{1,2,0:T(1,128)} %param.25) | copy-start | bytes 100
  9.8 66.2 %copy-start.5 = (bf16[1,128,1024]{2,1,0:T(8,128)(2,1)S(1)}, bf16[1,128,1024]{2,1,0:T(8,128)(2,1)}, u32[]{:S(2)}) copy-start(bf16[1,128,1024]{2,1,0:T(8,128)(2,1)} %param.14) | copy-start | bytes 786436
  9.8 66.4 %copy-start.14 = (s32[1,1,4]{2,1,0:T(1,128)S(1)}, s32[1,1,4]{2,1,0:T(1,128)}, u32[]{:S(2)}) copy-start(s32[1,1,4]{2,1,0:T(1,128)} %param.19) | copy-start | bytes 52
  9.8 66.5 %copy-start.6 = (bf16[1,128,1024]{2,1,0:T(8,128)(2,1)S(1)}, bf16[1,128,1024]{2,1,0:T(8,128)(2,1)}, u32[]{:S(2)}) copy-start(bf16[1,128,1024]{2,1,0:T(8,128)(2,1)} %param.15) | copy-start | bytes 786436
  9.8 84.0 %all-to-all-start = ((bf16[16,64,1024]{2,1,0:T(8,128)(2,1)}), bf16[16,64,1024]{2,1,0:T(8,128)(2,1)}, u32[]{:S(2)}, u32[]{:S(2)}) async-start(bf16[16,64,1024]{2,1,0:T(8,128)(2,1)} %broadcast_in_dim.111), calls=%async_computation | async-start | bytes 4194304 | tf_op jit(solution)/shard_map/all_to_all | solution.py:37
  18.7 97.1 %all-gather.2.cloned.1.call-start = ((), (), s32[]{:S(2)}) async-start(), calls=%async_computation.3 | async-start | bytes 2162688 | tf_op jit(solution)/shard_map/all_gather | solution.py:114
  99.3 2.2 copy-start.1
  101.7 2.3 copy-start.2
  104.0 1.6 copy-start.8
  105.6 10.3 %copy-start.7 = (bf16[1,128,1024]{2,1,0:T(8,128)(2,1)S(1)}, bf16[1,128,1024]{2,1,0:T(8,128)(2,1)}, u32[]{:S(2)}) copy-start(bf16[1,128,1024]{2,1,0:T(8,128)(2,1)} %param.13) | copy-start | bytes 786436
  105.6 12.4 %copy-start.4 = (pred[1280,128]{1,0:T(8,128)(4,1)S(1)}, pred[1280,128]{1,0:T(8,128)(4,1)}, u32[]{:S(2)}) copy-start(pred[1280,128]{1,0:T(8,128)(4,1)} %fusion.5) | copy-start | bytes 491524
  105.9 13.0 %copy-start.3 = (bf16[128,8,2,64]{0,3,2,1:T(8,128)(2,1)}, bf16[128,8,2,64]{0,3,2,1:T(8,128)(2,1)S(1)}, u32[]{:S(2)}) copy-start(bf16[128,8,2,64]{0,3,2,1:T(8,128)(2,1)S(1)} %fusion.23) | copy-start | bytes 786436
  187.0 2.9 %copy-start.12 = (bf16[1,512,1024]{2,1,0:T(8,128)(2,1)S(1)}, bf16[1,512,1024]{2,1,0:T(8,128)(2,1)}, u32[]{:S(2)}) copy-start(bf16[1,512,1024]{2,1,0:T(8,128)(2,1)} %param.24) | copy-start | bytes 3145732
  193.0 6.2 %copy-start.10 = (f32[1,128,8]{1,2,0:T(8,128)S(1)}, f32[1,128,8]{1,2,0:T(8,128)}, u32[]{:S(2)}) copy-start(f32[1,128,8]{1,2,0:T(8,128)} %param.22) | copy-start | bytes 12292
  193.0 67.0 %all-to-all-start.2 = ((bf16[32,40,1024]{2,1,0:T(8,128)(2,1)}), bf16[32,40,1024]{2,1,0:T(8,128)(2,1)}, u32[]{:S(2)}, u32[]{:S(2)}) async-start(bf16[32,40,1024]{2,1,0:T(8,128)(2,1)} %bitcast.122), calls=%async_computation.2 | async-start | bytes 5242880 | tf_op jit(solution)/shard_map/all_to_all | solution.py:144
Sparse Core Ops, SparseCore 0:
  22.9 92.8 all-gather.1

commit v5 on v2

--- a/solution.py
+++ b/solution.py
@@ -94,16 +94,18 @@
     keep_rows = jnp.repeat(block_keep[0], KB)
     position_abs = lax.axis_index("blk") * block_rows + jnp.arange(block_rows, dtype=jnp.int32)
     live_keys = ((keep_rows > 0) & (position_abs < prompt_lengths[0])).astype(jnp.int32)[None, :]
-    piece_kv = lax.all_gather(prompt_kv, "blk", axis=1, tiled=True)
+    keys_all = lax.all_gather(prompt_kv[0, :, :kv_width], "blk", axis=0, tiled=True)
+    values_local, keys_all = lax.optimization_barrier((prompt_kv[0, :, kv_width:], keys_all))
+    values_all = lax.all_gather(values_local, "blk", axis=0, tiled=True)
     blk_count = lax.axis_size("blk")
     page_count = block_rows // PAGE
     packed = jnp.concatenate([live_keys[0], page_owner[0, :, 0]])
     packed_all = lax.all_gather(packed, "blk", axis=0, tiled=True).reshape(blk_count, -1)
     piece_live = packed_all[:, :block_rows].reshape(1, -1)
     owners_all = packed_all[:, block_rows:]
-    count = piece_kv.shape[1]
-    key_heads = piece_kv[0, :, :kv_width].reshape(count, KVH, HD)
-    value_heads = piece_kv[0, :, kv_width:].reshape(count, KVH, HD)
+    count = keys_all.shape[0]
+    key_heads = keys_all.reshape(count, KVH, HD)
+    value_heads = values_all.reshape(count, KVH, HD)
     visible = (piece_live[0] > 0)[None, None, None, :]
     running_max, denom, numerator = absorb(
         carry_state, query_heads, key_heads, value_heads, visible
@@ -164,13 +166,14 @@
     page_slot = jnp.where(owners_all == me, block_of * page_capacity + page_rank, -1).reshape(-1)
     out_rows = blk_count * page_capacity * PAGE
     row_slot = jnp.arange(out_rows, dtype=jnp.int32) // PAGE
-    prompt_rows = piece_kv.shape[1]
+    prompt_rows = keys_all.shape[0]
     src_page = jnp.arange(prompt_rows, dtype=jnp.int32) // PAGE
     same_row = (jnp.arange(out_rows)[:, None] % PAGE) == (jnp.arange(prompt_rows)[None, :] % PAGE)
     chooser = (page_slot[src_page][None, :] == row_slot[:, None]) & same_row
-    cache_pages = jnp.dot(
-        chooser.astype(jnp.bfloat16), piece_kv[0], preferred_element_type=jnp.float32
-    ).astype(jnp.bfloat16)[None]
+    chooser = chooser.astype(jnp.bfloat16)
+    cache_keys = jnp.dot(chooser, keys_all, preferred_element_type=jnp.float32)
+    cache_values = jnp.dot(chooser, values_all, preferred_element_type=jnp.float32)
+    cache_pages = jnp.concatenate([cache_keys, cache_values], axis=1).astype(jnp.bfloat16)[None]
     return (attended[None], layer_out[None], cache_pages)
 
 

time: 265 us -> 326 us (1.23)
  waiting for transfers between devices: 69.8 us -> 126 us
  matrix products: 21.3 us -> 24.8 us
    all_gather x1 -> x2, waiting for transfers between devices: 22.4 us -> 80.7 us  [the longest x1 61.2 us: local(): values_all = lax.all_gather(values_local, 'blk', axis=0, tiled=True)]
    slice x5 -> x3, local copies, waits for them, and re-layouts: 5.76 us -> 1.88 us  [the longest x1 1.67 us: local(): prompt_kv[0, :, :kv_width]]
  transfers between devices with their start and end apart: 3 -> 4, of which waited for: 2 -> 3; matrix products, arithmetic and copies ran while one was open for 18% -> 16% of each run, Pallas kernels for 0% -> 0%
where the time goes in v5:
time: 326 us
  waiting for transfers between devices  126 us (39%)
  blocking collectives  96.2 us (30%)
  matrix products  24.8 us (8%)
  other arithmetic  21.3 us (7%)
  local copies, waits for them, and re-layouts  20.6 us (6%)
  starting transfers between devices  20.6 us (6%)
  between operations  15.9 us (5%)
    all_to_all x1, blocking collectives, local(): lax.all_to_all(dispatch, 'exp', split_axis=0, concat_axis=0, tiled=True)  82.2 us
    all_gather x1, waiting for transfers between devices, local(): values_all = lax.all_gather(values_local, 'blk', axis=0, tiled=True)  61.2 us
    all_to_all x1, waiting for transfers between devices, local(): lax.all_to_all(outgoing, 'exp', split_axis=0, concat_axis=0, tiled=True)  45.6 us
    all_gather x1, waiting for transfers between devices, local(): lax.all_gather(prompt_kv[0, :, :kv_width], 'blk', axis=0, tiled=True)  19.5 us
    all_to_all x1, starting transfers between devices, gather_rows(): whole = lax.all_to_all(tiles, axis, split_axis=0, concat_axis=0, tiled=True)  14.5 us
    unnamed x1, blocking collectives  14 us
    another operation x4, other arithmetic  9.3 us
    gather x1, local copies, waits for them, and re-layouts, local(): chooser = (page_slot[src_page][None, :] == row_slot[:, None]) & same_row  6.57 us
  transfers between devices with their start and end apart: 4, of which 3 were waited for; matrix products, arithmetic and copies ran while one was open for 16% of the time, Pallas kernels for 0%

profile of v5, /device:TPU:1, one launch (start us, length us, event | category | flops | bytes accessed | tf_op | source)
XLA Modules:
  0.0 325.8 jit_solution(281430683798191706)
XLA Ops:
  7.3 1.7 fusion.61
  9.0 2.4 broadcast_in_dim.109
  11.4 14.5 %all-to-all-start = ((bf16[32,32,1024]{2,1,0:T(8,128)(2,1)}), bf16[32,32,1024]{2,1,0:T(8,128)(2,1)}, u32[]{:S(2)}, u32[]{:S(2)}) async-start(bf16[32,32,1024]{2,1,0:T(8,128)(2,1)} %broadcast_in_dim.109), calls=%async_computation | async-start | bytes 4194304 | tf_op jit(solution)/shard_map/all_to_all | solution.py:37
  26.8 1.3 dynamic-slice
  28.9 14.0 %all-reduce = s32[1152]{0:T(1024)S(1)} all-reduce(s32[1152]{0:T(1024)S(1)} %add_dynamic-update-slice_fusion), channel_id=1, replica_groups=mesh['blk'=16,'exp'=32] {'blk'}, use_global_device_ids=true, to_apply=%add | all-reduce | flops 1152 | bytes 9216
  43.8 0.8 copy.56
  44.6 0.8 copy.58
  45.3 9.0 %reduce-window.19 = s32[32,8,128]{2,1,0:T(8,128)S(1)} reduce-window(s32[32,8,128]{2,1,0:T(8,128)S(1)} %fusion.47, s32[]{:T(128)} %constant.83.clone.1), window={size=1x1x128 pad=0_0x0_0x127_0}, to_apply=%region_6.7 | reduce-window | flops 4161536 | bytes 262148 | tf_op jit(solution)/shard_map/reduce-window.1
  55.1 5.3 %fusion.5 = pred[1280,128]{1,0:T(8,128)(4,1)} fusion(s32[128,8]{0,1:T(8,128)S(1)} %copy.69), kind=kLoop, calls=%fused_computation.11 | loop fusion | flops 2457600 | bytes 167936 | tf_op jit(solution)/shard_map/reduce_or | solution.py:132
  60.5 19.5 %all-gather.6.cloned.1.call-done = bf16[1,1024,512]{2,1,0:T(8,128)(2,1)} async-done(((bf16[1,64,512]{2,1,0:T(8,128)(2,1)}), bf16[1,1024,512]{2,1,0:T(8,128)(2,1)}) %all-gather.6.cloned.1.call-update) | async-done | bytes 1048592 | tf_op jit(solution)/shard_map/all_gather | solution.py:97
  80.0 1.5 copy.60
  81.5 1.4 select_reduce_fusion.1
  83.0 2.2 fusion
  85.5 2.2 fusion.3
  87.7 0.8 copy-done.1
  89.0 61.2 %all-gather.4.cloned.1.call-done = bf16[1024,512]{1,0:T(8,128)(2,1)} async-done(((bf16[64,512]{1,0:T(8,128)(2,1)}), bf16[1024,512]{1,0:T(8,128)(2,1)}) %all-gather.4.cloned.1.call-update) | async-done | bytes 1048592 | tf_op jit(solution)/shard_map/all_gather | solution.py:99
  150.2 1.5 copy.61
  151.8 4.6 %fusion.14 = f32[128,8,2,64]{0,3,2,1:T(8,128)S(1)} fusion(bf16[1024,8,64,1]{0,2,3,1:T(8,128)(2,1)S(1)} %bitcast.131, f32[8,1024,128,2]{2,1,3,0:T(8,128)} %copy-done.1, f32[128,8,2]{0,2,1:T(2,128)S(1)} %get-tuple-element.26, pred[1024]{0:T(1024)(128)(4,1)S(1)} %gt.28), kind=kOutput, calls=%fused_computation.23 | convolution fusion | flops 276824064 | bytes 9970688 | tf_op jit(solution)/shard_map/tkgs,skd->tkgd/dot_general | solution.py:51
  156.8 2.2 multiply_reduce_fusion
  159.0 0.9 convolution_convert_fusion.1
  159.9 82.2 %all_to_all.15 = bf16[32,40,1024]{2,1,0:T(8,128)(2,1)S(1)} all-to-all(bf16[32,40,1024]{2,1,0:T(8,128)(2,1)S(1)} %bitcast.124), channel_id=1, replica_groups=mesh['blk'=16,'exp'=32] {'exp'}, dimensions={0} | all-to-all | bytes 5242880 | tf_op jit(solution)/shard_map/all_to_all | solution.py:135
  242.2 2.9 fusion.10
  245.1 3.1 convolution_convert_fusion
  248.3 6.0 %all-to-all-start.2 = ((bf16[32,40,1024]{2,1,0:T(8,128)(2,1)}), bf16[32,40,1024]{2,1,0:T(8,128)(2,1)}, u32[]{:S(2)}, u32[]{:S(2)}) async-start(bf16[32,40,1024]{2,1,0:T(8,128)(2,1)} %bitcast.127), calls=%async_computation.2 | async-start | bytes 5242880 | tf_op jit(solution)/shard_map/all_to_all | solution.py:146
  255.3 6.6 %gather_fusion = s32[1024]{0:T(1024)S(1)} fusion(s32[128]{0:T(128)S(1)} %reshape.317, s32[1024]{0:T(1024)S(1)} %broadcast_clamp_fusion), kind=kCustom, calls=%fused_computation | custom fusion | bytes 12288 | tf_op jit(solution)/shard_map/gather | solution.py:172
  261.9 1.6 select_reduce_fusion
  263.6 1.7 fusion.25
  265.3 1.8 copy.70
  267.1 1.7 fusion.26
  268.8 0.9 pad_maximum_fusion
  269.7 45.6 %all-to-all-done.2 = bf16[32,40,1024]{2,1,0:T(8,128)(2,1)} async-done(((bf16[32,40,1024]{2,1,0:T(8,128)(2,1)}), bf16[32,40,1024]{2,1,0:T(8,128)(2,1)}, u32[]{:S(2)}, u32[]{:S(2)}) %all-to-all-start.2) | async-done | bytes 2621472 | tf_op jit(solution)/shard_map/all_to_all | solution.py:146
  315.3 3.7 %fusion.27 = bf16[1,128,1024]{2,1,0:T(8,128)(2,1)} fusion(f32[128,1024]{1,0:T(8,128)S(1)} %get-tuple-element.33, f32[128,1280]{1,0:T(8,128)S(1)} %select_reduce_fusion, bf16[1280,1024]{1,0:T(8,128)(2,1)} %bitcast.39), kind=kOutput, calls=%fused_computation.38 | convolution fusion | flops 2013528064 | bytes 4063232 | tf_op jit(solution)/shard_map/dot_general | solution.py:155
  (89 shorter events, 4.4 us)
Async XLA Ops:
  7.2 235.0 %copy-start = (bf16[1,1024,1024]{2,1,0:T(8,128)(2,1)S(1)}, bf16[1,1024,1024]{2,1,0:T(8,128)(2,1)}, u32[]{:S(2)}) copy-start(bf16[1,1024,1024]{2,1,0:T(8,128)(2,1)} %param.23) | copy-start | bytes 6291460
  7.2 18.7 %copy-start.17 = (s32[1,2]{1,0:T(1,128)S(1)}, s32[1,2]{1,0:T(1,128)}, u32[]{:S(2)}) copy-start(s32[1,2]{1,0:T(1,128)} %param.18) | copy-start | bytes 28
  7.2 21.5 %copy-start.15 = (s32[1,8,1]{1,2,0:T(1,128)S(1)}, s32[1,8,1]{1,2,0:T(1,128)}, u32[]{:S(2)}) copy-start(s32[1,8,1]{1,2,0:T(1,128)} %param.25) | copy-start | bytes 100
  7.2 35.8 %copy-start.13 = (s32[1,128,8]{1,2,0:T(8,128)S(1)}, s32[1,128,8]{1,2,0:T(8,128)}, u32[]{:S(2)}) copy-start(s32[1,128,8]{1,2,0:T(8,128)} %param.21) | copy-start | bytes 12292
  7.2 36.0 %copy-start.7 = (bf16[1,128,1024]{2,1,0:T(8,128)(2,1)S(1)}, bf16[1,128,1024]{2,1,0:T(8,128)(2,1)}, u32[]{:S(2)}) copy-start(bf16[1,128,1024]{2,1,0:T(8,128)(2,1)} %param.15) | copy-start | bytes 786436
  7.2 36.2 %copy-start.8 = (bf16[1,128,1024]{2,1,0:T(8,128)(2,1)S(1)}, bf16[1,128,1024]{2,1,0:T(8,128)(2,1)}, u32[]{:S(2)}) copy-start(bf16[1,128,1024]{2,1,0:T(8,128)(2,1)} %param.14) | copy-start | bytes 786436
  7.2 36.4 %copy-start.18 = (s32[1,1,4]{2,1,0:T(1,128)S(1)}, s32[1,1,4]{2,1,0:T(1,128)}, u32[]{:S(2)}) copy-start(s32[1,1,4]{2,1,0:T(1,128)} %param.19) | copy-start | bytes 52
  7.2 72.8 %all-gather.6.cloned.1.call-start = ((), (), s32[]{:S(2)}) async-start(), calls=%async_computation.4 | async-start | bytes 1114112 | tf_op jit(solution)/shard_map/all_gather | solution.py:97
  11.4 145.4 %all-to-all-start = ((bf16[32,32,1024]{2,1,0:T(8,128)(2,1)}), bf16[32,32,1024]{2,1,0:T(8,128)(2,1)}, u32[]{:S(2)}, u32[]{:S(2)}) async-start(bf16[32,32,1024]{2,1,0:T(8,128)(2,1)} %broadcast_in_dim.109), calls=%async_computation | async-start | bytes 4194304 | tf_op jit(solution)/shard_map/all_to_all | solution.py:37
  25.9 124.4 %all-gather.4.cloned.1.call-start = ((), (), s32[]{:S(2)}) async-start(), calls=%async_computation.3 | async-start | bytes 1114112 | tf_op jit(solution)/shard_map/all_gather | solution.py:99
  81.5 3.7 %copy-start.2 = (bf16[1,1024,512]{1,2,0:T(8,128)(2,1)}, bf16[1,1024,512]{1,2,0:T(8,128)(2,1)S(1)}, u32[]{:S(2)}) copy-start(bf16[1,1024,512]{1,2,0:T(8,128)(2,1)S(1)} %copy.60) | copy-start | bytes 3145732
  82.9 2.3 copy-start.3
  85.2 3.2 copy-start.1
  151.7 4.7 %copy-start.4 = (f32[128,8,2,128]{0,3,2,1:T(8,128)S(1)}, f32[128,8,2,128]{0,3,2,1:T(8,128)}, u32[]{:S(2)}) copy-start(f32[128,8,2,128]{0,3,2,1:T(8,128)} %copy-done.3) | copy-start | bytes 3145732
  151.7 4.7 %copy-start.10 = (bf16[1,128,512]{1,2,0:T(8,128)(2,1)S(1)}, bf16[1,128,512]{1,2,0:T(8,128)(2,1)}, u32[]{:S(2)}) copy-start(bf16[1,128,512]{1,2,0:T(8,128)(2,1)} %copy.58) | copy-start | bytes 393220
  151.8 4.7 %copy-start.11 = (f32[128,8,2]{0,2,1:T(2,128)S(1)}, f32[128,8,2]{0,2,1:T(2,128)}, u32[]{:S(2)}) copy-start(f32[128,8,2]{0,2,1:T(2,128)} %get-tuple-element.19) | copy-start | bytes 24580
  151.8 4.7 %copy-start.12 = (f32[128,8,2]{0,2,1:T(2,128)S(1)}, f32[128,8,2]{0,2,1:T(2,128)}, u32[]{:S(2)}) copy-start(f32[128,8,2]{0,2,1:T(2,128)} %get-tuple-element.20) | copy-start | bytes 24580
  151.8 5.0 %copy-start.9 = (bf16[1,128,1024]{2,1,0:T(8,128)(2,1)S(1)}, bf16[1,128,1024]{2,1,0:T(8,128)(2,1)}, u32[]{:S(2)}) copy-start(bf16[1,128,1024]{2,1,0:T(8,128)(2,1)} %param.13) | copy-start | bytes 786436
  156.4 2.6 copy-start.6
  156.8 85.4 %copy-start.5 = (bf16[128,8,2,64]{0,3,2,1:T(8,128)(2,1)}, bf16[128,8,2,64]{0,3,2,1:T(8,128)(2,1)S(1)}, u32[]{:S(2)}) copy-start(bf16[128,8,2,64]{0,3,2,1:T(8,128)(2,1)S(1)} %fusion.22) | copy-start | bytes 786436
  242.2 2.9 copy-start.16
  248.3 6.2 %copy-start.14 = (f32[1,128,8]{1,2,0:T(8,128)S(1)}, f32[1,128,8]{1,2,0:T(8,128)}, u32[]{:S(2)}) copy-start(f32[1,128,8]{1,2,0:T(8,128)} %param.22) | copy-start | bytes 12292
  248.3 67.0 %all-to-all-start.2 = ((bf16[32,40,1024]{2,1,0:T(8,128)(2,1)}), bf16[32,40,1024]{2,1,0:T(8,128)(2,1)}, u32[]{:S(2)}, u32[]{:S(2)}) async-start(bf16[32,40,1024]{2,1,0:T(8,128)(2,1)} %bitcast.127), calls=%async_computation.2 | async-start | bytes 5242880 | tf_op jit(solution)/shard_map/all_to_all | solution.py:146
Sparse Core Ops, SparseCore 0:
  10.2 69.7 all-gather.5
  82.1 68.1 all-gather.3

commit v6 on v2

--- a/solution.py
+++ b/solution.py
@@ -150,11 +150,11 @@
         ),
         axis=1,
     )
-    combined = jnp.dot(
-        slot_weight,
-        returned.reshape(experts * capacity, D).astype(jnp.float32),
-        precision=lax.Precision.HIGHEST,
-        preferred_element_type=jnp.float32,
+    weight_hi = slot_weight.astype(jnp.bfloat16)
+    weight_lo = (slot_weight - weight_hi.astype(jnp.float32)).astype(jnp.bfloat16)
+    returned_rows = returned.reshape(experts * capacity, D)
+    combined = jnp.dot(weight_hi, returned_rows, preferred_element_type=jnp.float32) + jnp.dot(
+        weight_lo, returned_rows, preferred_element_type=jnp.float32
     )
     layer_out = (stream_f32 + combined).astype(jnp.bfloat16)
     page_capacity = max(2, 2 * page_count // blk_count)

time: 265 us -> 266 us (level)
  no operation moved by 1% of the time
where the time goes in v6:
time: 266 us; the launch traced here: 265 us
  blocking collectives  95.7 us (36%)
  waiting for transfers between devices  69.8 us (26%)
  matrix products  22.8 us (9%)
  local copies, waits for them, and re-layouts  20.7 us (8%)
  starting transfers between devices  20.7 us (8%)
  other arithmetic  19.9 us (7%)
  between operations  15.8 us (6%)
    all_to_all x1, blocking collectives, local(): lax.all_to_all(dispatch, 'exp', split_axis=0, concat_axis=0, tiled=True)  81 us
    all_to_all x1, waiting for transfers between devices, local(): lax.all_to_all(outgoing, 'exp', split_axis=0, concat_axis=0, tiled=True)  46.7 us
    all_gather x1, waiting for transfers between devices, local(): piece_kv = lax.all_gather(prompt_kv, 'blk', axis=1, tiled=True)  22.4 us
    unnamed x1, blocking collectives  14.7 us
    all_to_all x1, starting transfers between devices, gather_rows(): whole = lax.all_to_all(tiles, axis, split_axis=0, concat_axis=0, tiled=True)  14.6 us
    another operation x4, other arithmetic  9.33 us
    gather x1, local copies, waits for them, and re-layouts, local(): chooser = (page_slot[src_page][None, :] == row_slot[:, None]) & same_row  6.57 us
    all_to_all x1, starting transfers between devices, local(): lax.all_to_all(outgoing, 'exp', split_axis=0, concat_axis=0, tiled=True)  6 us
  transfers between devices with their start and end apart: 3, of which 2 were waited for; matrix products, arithmetic and copies ran while one was open for 18% of the time, Pallas kernels for 0%

profile of v6, /device:TPU:1, one launch (start us, length us, event | category | flops | bytes accessed | tf_op | source)
XLA Modules:
  0.0 265.3 jit_solution(3860407156505130534)
XLA Ops:
  7.2 0.7 all-gather.2.cloned.1.call-update
  7.9 2.4 broadcast_in_dim.111
  10.3 14.6 %all-to-all-start = ((bf16[32,32,1024]{2,1,0:T(8,128)(2,1)}), bf16[32,32,1024]{2,1,0:T(8,128)(2,1)}, u32[]{:S(2)}, u32[]{:S(2)}) async-start(bf16[32,32,1024]{2,1,0:T(8,128)(2,1)} %broadcast_in_dim.111), calls=%async_computation | async-start | bytes 4194304 | tf_op jit(solution)/shard_map/all_to_all | solution.py:37
  26.1 1.3 dynamic-slice
  28.3 14.7 %all-reduce = s32[1152]{0:T(1024)S(1)} all-reduce(s32[1152]{0:T(1024)S(1)} %add_dynamic-update-slice_fusion), channel_id=1, replica_groups=mesh['blk'=16,'exp'=32] {'blk'}, use_global_device_ids=true, to_apply=%add | all-reduce | flops 1152 | bytes 9216
  43.7 0.8 copy.44
  44.4 9.0 %reduce-window.19 = s32[32,8,128]{2,1,0:T(8,128)S(1)} reduce-window(s32[32,8,128]{2,1,0:T(8,128)S(1)} %fusion.56, s32[]{:T(128)} %constant.83.clone.1), window={size=1x1x128 pad=0_0x0_0x127_0}, to_apply=%region_6.7 | reduce-window | flops 4161536 | bytes 262148 | tf_op jit(solution)/shard_map/reduce-window.1
  54.2 5.3 %fusion.5 = pred[1280,128]{1,0:T(8,128)(4,1)} fusion(s32[128,8]{0,1:T(8,128)S(1)} %copy.55), kind=kLoop, calls=%fused_computation.11 | loop fusion | flops 2457600 | bytes 167936 | tf_op jit(solution)/shard_map/reduce_or | solution.py:130
  59.6 1.3 select_reduce_fusion.1
  60.9 22.4 %all-gather.2.cloned.1.call-done = bf16[1,1024,1024]{2,1,0:T(8,128)(2,1)} async-done(((bf16[1,64,1024]{2,1,0:T(8,128)(2,1)}), bf16[1,1024,1024]{2,1,0:T(8,128)(2,1)}) %all-gather.2.cloned.1.call-update) | async-done | bytes 2097168 | tf_op jit(solution)/shard_map/all_gather | solution.py:97
  83.3 2.7 %fusion.69 = (bf16[1,1024,512]{2,1,0:T(8,128)(2,1)}, bf16[1,1024,512]{2,1,0:T(8,128)(2,1)S(1)}) fusion(bf16[1,1024,1024]{2,1,0:T(8,128)(2,1)} %all-gather.2.cloned.1.call-done), kind=kLoop, calls=%fused_computation.113 | loop fusion | bytes 4194304 | tf_op jit(solution)/shard_map/slice | solution.py:105
  86.1 1.3 copy.47
  87.4 1.5 copy.46
  88.9 2.2 fusion
  91.3 2.2 fusion.3
  93.6 1.5 fusion.22
  95.2 0.3 fusion.31
  95.5 0.6 copy-done.7
  96.1 2.1 multiply_reduce_fusion
  98.3 0.9 convolution_convert_fusion.1
  99.2 81.0 %all_to_all.15 = bf16[32,40,1024]{2,1,0:T(8,128)(2,1)S(1)} all-to-all(bf16[32,40,1024]{2,1,0:T(8,128)(2,1)S(1)} %bitcast.124), channel_id=1, replica_groups=mesh['blk'=16,'exp'=32] {'exp'}, dimensions={0} | all-to-all | bytes 5242880 | tf_op jit(solution)/shard_map/all_to_all | solution.py:133
  180.2 2.9 %fusion.12 = f32[1280,1024]{1,0:T(8,128)S(1)} fusion(bf16[1280,1024]{1,0:T(8,128)(2,1)S(1)} %bitcast.127, bf16[1,1024,1024]{2,1,0:T(8,128)(2,1)S(1)} %copy-done), kind=kOutput, calls=%fused_computation.20 | convolution fusion | flops 2684354560 | bytes 9961472 | tf_op jit(solution)/shard_map/dot_general | solution.py:137
  183.1 3.1 %convolution_convert_fusion = bf16[1280,1024]{1,0:T(8,128)(2,1)} fusion(f32[1280,1024]{1,0:T(8,128)S(1)} %fusion.12, bf16[1,512,1024]{2,1,0:T(8,128)(2,1)S(1)} %copy-done.12), kind=kOutput, calls=%fused_computation.14 | convolution fusion | flops 1347420160 | bytes 8912896 | tf_op jit(solution)/shard_map/dot_general | solution.py:139
  186.3 6.0 %all-to-all-start.2 = ((bf16[32,40,1024]{2,1,0:T(8,128)(2,1)}), bf16[32,40,1024]{2,1,0:T(8,128)(2,1)}, u32[]{:S(2)}, u32[]{:S(2)}) async-start(bf16[32,40,1024]{2,1,0:T(8,128)(2,1)} %bitcast.126), calls=%async_computation.2 | async-start | bytes 5242880 | tf_op jit(solution)/shard_map/all_to_all | solution.py:144
  192.7 0.4 select_reduce_fusion.2
  193.3 6.6 %gather_fusion = s32[1024]{0:T(1024)S(1)} fusion(s32[128]{0:T(128)S(1)} %reshape.278, s32[1024]{0:T(1024)S(1)} %broadcast_clamp_fusion), kind=kCustom, calls=%fused_computation | custom fusion | bytes 12288 | tf_op jit(solution)/shard_map/gather | solution.py:170
  199.9 1.6 select_reduce_fusion
  201.6 1.8 copy.56
  203.4 3.1 %fusion.19 = bf16[1,256,1024]{2,1,0:T(8,128)(2,1)} fusion(bf16[1,1024,1024]{2,1,0:T(8,128)(2,1)} %all-gather.2.cloned.1.call-done, s32[1024]{0:T(1024)S(1)} %add_select_fusion.1, s32[1024]{0:T(1024)S(1)} %gather_fusion, s32[256]{0:T(256)S(1)} %get-tuple-element.27, s32[256]{0:T(256)S(1)} %get-tuple-element.28), kind=kOutput, calls=%fused_computation.25 | convolution fusion | flops 537919488 | bytes 2631680 | tf_op jit(solution)/shard_map/dot_general | solution.py:171
  206.5 46.7 %all-to-all-done.2 = bf16[32,40,1024]{2,1,0:T(8,128)(2,1)} async-done(((bf16[32,40,1024]{2,1,0:T(8,128)(2,1)}), bf16[32,40,1024]{2,1,0:T(8,128)(2,1)}, u32[]{:S(2)}, u32[]{:S(2)}) %all-to-all-start.2) | async-done | bytes 2621472 | tf_op jit(solution)/shard_map/all_to_all | solution.py:144
  253.3 2.2 fusion.51
  255.5 3.0 %fusion.34 = bf16[1,128,1024]{2,1,0:T(8,128)(2,1)} fusion(f32[128,1024]{1,0:T(8,128)S(1)} %get-tuple-element.26, f32[128,1024]{1,0:T(8,128)S(1)} %fusion.51, bf16[1280,1024]{1,0:T(8,128)(2,1)} %bitcast.37, f32[128,1280]{1,0:T(8,128)S(1)} %select_reduce_fusion), kind=kOutput, calls=%fused_computation.39 | convolution fusion | flops 336592896 | bytes 4587520 | tf_op jit(solution)/shard_map/dot_general | solution.py:156
  (77 shorter events, 3.1 us)
Async XLA Ops:
  7.2 173.0 %copy-start = (bf16[1,1024,1024]{2,1,0:T(8,128)(2,1)S(1)}, bf16[1,1024,1024]{2,1,0:T(8,128)(2,1)}, u32[]{:S(2)}) copy-start(bf16[1,1024,1024]{2,1,0:T(8,128)(2,1)} %param.23) | copy-start | bytes 6291460
  7.2 76.1 %all-gather.2.cloned.1.call-start = ((), (), s32[]{:S(2)}) async-start(), calls=%async_computation.3 | async-start | bytes 2228224 | tf_op jit(solution)/shard_map/all_gather | solution.py:97
  10.3 14.7 %copy-start.9 = (s32[1,128,8]{1,2,0:T(8,128)S(1)}, s32[1,128,8]{1,2,0:T(8,128)}, u32[]{:S(2)}) copy-start(s32[1,128,8]{1,2,0:T(8,128)} %param.21) | copy-start | bytes 12292
  10.3 15.0 %copy-start.13 = (s32[1,2]{1,0:T(1,128)S(1)}, s32[1,2]{1,0:T(1,128)}, u32[]{:S(2)}) copy-start(s32[1,2]{1,0:T(1,128)} %param.18) | copy-start | bytes 28
  10.3 17.8 %copy-start.11 = (s32[1,8,1]{1,2,0:T(1,128)S(1)}, s32[1,8,1]{1,2,0:T(1,128)}, u32[]{:S(2)}) copy-start(s32[1,8,1]{1,2,0:T(1,128)} %param.25) | copy-start | bytes 100
  10.3 32.8 %copy-start.5 = (bf16[1,128,1024]{2,1,0:T(8,128)(2,1)S(1)}, bf16[1,128,1024]{2,1,0:T(8,128)(2,1)}, u32[]{:S(2)}) copy-start(bf16[1,128,1024]{2,1,0:T(8,128)(2,1)} %param.14) | copy-start | bytes 786436
  10.3 33.0 %copy-start.14 = (s32[1,1,4]{2,1,0:T(1,128)S(1)}, s32[1,1,4]{2,1,0:T(1,128)}, u32[]{:S(2)}) copy-start(s32[1,1,4]{2,1,0:T(1,128)} %param.19) | copy-start | bytes 52
  10.3 33.2 %copy-start.6 = (bf16[1,128,1024]{2,1,0:T(8,128)(2,1)S(1)}, bf16[1,128,1024]{2,1,0:T(8,128)(2,1)}, u32[]{:S(2)}) copy-start(bf16[1,128,1024]{2,1,0:T(8,128)(2,1)} %param.15) | copy-start | bytes 786436
  10.3 85.2 %all-to-all-start = ((bf16[32,32,1024]{2,1,0:T(8,128)(2,1)}), bf16[32,32,1024]{2,1,0:T(8,128)(2,1)}, u32[]{:S(2)}, u32[]{:S(2)}) async-start(bf16[32,32,1024]{2,1,0:T(8,128)(2,1)} %broadcast_in_dim.111), calls=%async_computation | async-start | bytes 4194304 | tf_op jit(solution)/shard_map/all_to_all | solution.py:37
  88.9 2.2 copy-start.1
  91.3 2.3 copy-start.2
  93.6 1.6 copy-start.8
  95.2 1.0 copy-start.7
  95.2 3.1 %copy-start.4 = (pred[1280,128]{1,0:T(8,128)(4,1)S(1)}, pred[1280,128]{1,0:T(8,128)(4,1)}, u32[]{:S(2)}) copy-start(pred[1280,128]{1,0:T(8,128)(4,1)} %fusion.5) | copy-start | bytes 491524
  95.5 3.7 %copy-start.3 = (bf16[128,8,2,64]{0,3,2,1:T(8,128)(2,1)}, bf16[128,8,2,64]{0,3,2,1:T(8,128)(2,1)S(1)}, u32[]{:S(2)}) copy-start(bf16[128,8,2,64]{0,3,2,1:T(8,128)(2,1)S(1)} %fusion.31) | copy-start | bytes 786436
  180.2 2.9 %copy-start.12 = (bf16[1,512,1024]{2,1,0:T(8,128)(2,1)S(1)}, bf16[1,512,1024]{2,1,0:T(8,128)(2,1)}, u32[]{:S(2)}) copy-start(bf16[1,512,1024]{2,1,0:T(8,128)(2,1)} %param.24) | copy-start | bytes 3145732
  186.2 6.2 %copy-start.10 = (f32[1,128,8]{1,2,0:T(8,128)S(1)}, f32[1,128,8]{1,2,0:T(8,128)}, u32[]{:S(2)}) copy-start(f32[1,128,8]{1,2,0:T(8,128)} %param.22) | copy-start | bytes 12292
  186.3 67.0 %all-to-all-start.2 = ((bf16[32,40,1024]{2,1,0:T(8,128)(2,1)}), bf16[32,40,1024]{2,1,0:T(8,128)(2,1)}, u32[]{:S(2)}, u32[]{:S(2)}) async-start(bf16[32,40,1024]{2,1,0:T(8,128)(2,1)} %bitcast.126), calls=%async_computation.2 | async-start | bytes 5242880 | tf_op jit(solution)/shard_map/all_to_all | solution.py:144
Sparse Core Ops, SparseCore 0:
  10.1 73.1 all-gather.1

commit v7 on v2

--- a/solution.py
+++ b/solution.py
@@ -2,6 +2,7 @@
 import jax.numpy as jnp
 from jax import lax
 from jax.sharding import PartitionSpec as P
+from jax.experimental import pallas as pl
 
 D = 1024
 H = 16
@@ -36,6 +37,33 @@
     tiles = jnp.broadcast_to(piece[None], (count,) + piece.shape)
     whole = lax.all_to_all(tiles, axis, split_axis=0, concat_axis=0, tiled=True)
     return whole.reshape((count * piece.shape[0],) + piece.shape[1:])
+
+
+def prompt_attend_kernel(q_ref, kv_ref, live_ref, m_ref, l_ref, acc_ref, out_ref):
+    kv_width = KVH * HD
+    visible = live_ref[...] > 0
+    for h in range(H):
+        k = h // (H // KVH)
+        qh = q_ref[:, h * HD:(h + 1) * HD]
+        kh = kv_ref[:, k * HD:(k + 1) * HD]
+        vh = kv_ref[:, kv_width + k * HD:kv_width + (k + 1) * HD]
+        s = lax.dot_general(qh, kh, (((1,), (1,)), ((), ())), preferred_element_type=jnp.float32) * SCALE
+        m_old = m_ref[:, h:h + 1]
+        m_new = jnp.maximum(m_old, jnp.max(jnp.where(visible, s, NEGATIVE), axis=1, keepdims=True))
+        factor = jnp.exp(m_old - m_new)
+        w = jnp.where(visible, jnp.exp(s - m_new), 0.0)
+        l_new = l_ref[:, h:h + 1] * factor + jnp.sum(w, axis=1, keepdims=True)
+        added = jnp.dot(w.astype(jnp.bfloat16), vh, preferred_element_type=jnp.float32)
+        acc = acc_ref[:, h * HD:(h + 1) * HD] * factor + added
+        out_ref[:, h * HD:(h + 1) * HD] = (acc / l_new).astype(jnp.bfloat16)
+
+
+def prompt_attend(q, kv, live, m0, l0, acc0):
+    tok = q.shape[0]
+    return pl.pallas_call(
+        prompt_attend_kernel,
+        out_shape=jax.ShapeDtypeStruct((tok, H * HD), jnp.bfloat16),
+    )(q, kv, live, m0, l0, acc0)
 
 
 def absorb(carry_state, query_heads, key_heads, value_heads, visible):
@@ -101,14 +129,15 @@
     packed_all = lax.all_gather(packed, "blk", axis=0, tiled=True).reshape(blk_count, -1)
     piece_live = packed_all[:, :block_rows].reshape(1, -1)
     owners_all = packed_all[:, block_rows:]
-    count = piece_kv.shape[1]
-    key_heads = piece_kv[0, :, :kv_width].reshape(count, KVH, HD)
-    value_heads = piece_kv[0, :, kv_width:].reshape(count, KVH, HD)
-    visible = (piece_live[0] > 0)[None, None, None, :]
-    running_max, denom, numerator = absorb(
-        carry_state, query_heads, key_heads, value_heads, visible
-    )
-    attended = (numerator / denom[..., None]).reshape(tok_rows, H * HD).astype(jnp.bfloat16)
+    suffix_max, suffix_denom, suffix_numerator = carry_state
+    attended = prompt_attend(
+        queries[0],
+        piece_kv[0],
+        piece_live,
+        suffix_max.reshape(tok_rows, H),
+        suffix_denom.reshape(tok_rows, H),
+        suffix_numerator.reshape(tok_rows, H * HD),
+    )
     projected = jnp.dot(
         attended,
         gather_rows(out_weight, "exp"),

time: 265 us -> 274 us (1.034)
  Pallas kernels: 0 us -> 10.4 us
  waiting for transfers between devices: 69.8 us -> 79.2 us
  local copies, waits for them, and re-layouts: 20.7 us -> 15.8 us
  matrix products: 21.3 us -> 18.4 us
    pallas_call x0 -> x1, Pallas kernels: none -> 10.4 us  [prompt_attend(): pl.pallas_call(prompt_attend_kernel, out_shape=jax.ShapeDtypeStruct((tok,...]
    all_gather x1, waiting for transfers between devices: 22.4 us -> 30 us  [local(): piece_kv = lax.all_gather(prompt_kv, 'blk', axis=1, tiled=True)]
    slice x5 -> x2, local copies, waits for them, and re-layouts: 5.76 us -> 0.22 us  [the longest x2 4.23 us: local(): key_heads = piece_kv[0, :, :kv_width].reshape(count, KVH, HD)]
  transfers between devices with their start and end apart: 3 -> 3, of which waited for: 2 -> 2; matrix products, arithmetic and copies ran while one was open for 18% -> 13% of each run, Pallas kernels for 0% -> 4%
where the time goes in v7:
time: 274 us; the launch traced here: 273 us
  blocking collectives  95 us (35%)
  waiting for transfers between devices  79.2 us (29%)
  starting transfers between devices  20.8 us (8%)
  matrix products  18.4 us (7%)
  other arithmetic  17.8 us (6%)
  local copies, waits for them, and re-layouts  15.8 us (6%)
  between operations  15.6 us (6%)
  Pallas kernels  10.4 us (4%)
    all_to_all x1, blocking collectives, local(): lax.all_to_all(dispatch, 'exp', split_axis=0, concat_axis=0, tiled=True)  81 us
    all_to_all x1, waiting for transfers between devices, local(): lax.all_to_all(outgoing, 'exp', split_axis=0, concat_axis=0, tiled=True)  48.5 us
    all_gather x1, waiting for transfers between devices, local(): piece_kv = lax.all_gather(prompt_kv, 'blk', axis=1, tiled=True)  30 us
    all_to_all x1, starting transfers between devices, gather_rows(): whole = lax.all_to_all(tiles, axis, split_axis=0, concat_axis=0, tiled=True)  14.6 us
    unnamed x1, blocking collectives  14 us
    pallas_call x1, Pallas kernels, prompt_attend(): pl.pallas_call(prompt_attend_kernel, out_shape=jax.ShapeDtypeStruct((tok,...  10.4 us
    another operation x4, other arithmetic  9.33 us
    gather x1, local copies, waits for them, and re-layouts, local(): chooser = (page_slot[src_page][None, :] == row_slot[:, None]) & same_row  6.57 us
  transfers between devices with their start and end apart: 3, of which 2 were waited for; matrix products, arithmetic and copies ran while one was open for 13% of the time, Pallas kernels for 4%

profile of v7, /device:TPU:1, one launch (start us, length us, event | category | flops | bytes accessed | tf_op | source)
XLA Modules:
  0.0 272.9 jit_solution(6331598782001752374)
XLA Ops:
  7.2 2.5 broadcast_in_dim.95
  9.8 14.6 %all-to-all-start = ((bf16[32,32,1024]{2,1,0:T(8,128)(2,1)}), bf16[32,32,1024]{2,1,0:T(8,128)(2,1)}, u32[]{:S(2)}, u32[]{:S(2)}) async-start(bf16[32,32,1024]{2,1,0:T(8,128)(2,1)} %broadcast_in_dim.95), calls=%async_computation | async-start | bytes 4194304 | tf_op jit(solution)/shard_map/all_to_all | solution.py:38
  24.4 0.7 all-gather.2.cloned.1.call-update
  26.3 1.3 dynamic-slice
  28.2 0.2 reduce-window.18
  28.4 0.2 add_dynamic-update-slice_fusion
  28.6 14.0 %all-reduce = s32[1152]{0:T(1024)S(1)} all-reduce(s32[1152]{0:T(1024)S(1)} %add_dynamic-update-slice_fusion), channel_id=1, replica_groups=mesh['blk'=16,'exp'=32] {'blk'}, use_global_device_ids=true, to_apply=%add | all-reduce | flops 1152 | bytes 9216
  42.6 0.7 reshape.242.live_ref
  43.3 9.0 %reduce-window.19 = s32[32,8,128]{2,1,0:T(8,128)S(1)} reduce-window(s32[32,8,128]{2,1,0:T(8,128)S(1)} %fusion.30, s32[]{:T(128)} %constant.81.clone.1), window={size=1x1x128 pad=0_0x0_0x127_0}, to_apply=%region_4.5 | reduce-window | flops 4161536 | bytes 262148 | tf_op jit(solution)/shard_map/reduce-window.1
  52.4 0.1 copy.67
  53.0 0.9 copy.56
  53.9 0.1 copy.60
  54.3 1.3 select_reduce_fusion.1
  55.7 1.1 fusion.7
  56.8 2.0 copy.63.acc_ref
  58.8 0.2 fusion.17
  59.2 4.8 %fusion = pred[1280,128]{1,0:T(8,128)(4,1)S(1)} fusion(s32[128,8]{0,1:T(8,128)S(1)} %copy.70), kind=kLoop, calls=%fused_computation.4 | loop fusion | flops 2457600 | bytes 167936 | tf_op jit(solution)/shard_map/reduce_or | solution.py:159
  64.1 0.6 multiply_add_fusion.l_ref
  64.7 30.0 %all-gather.2.cloned.1.call-done = bf16[1,1024,1024]{2,1,0:T(8,128)(2,1)} async-done(((bf16[1,64,1024]{2,1,0:T(8,128)(2,1)}), bf16[1,1024,1024]{2,1,0:T(8,128)(2,1)}) %all-gather.2.cloned.1.call-update) | async-done | bytes 2097168 | tf_op jit(solution)/shard_map/all_gather | solution.py:125
  94.7 10.4 %shard_map.148 = bf16[128,1024]{1,0:T(8,128)(2,1)} custom-call(bf16[128,1024]{1,0:T(8,128)(2,1)} %bitcast.90, bf16[1024,1024]{1,0:T(8,128)(2,1)} %bitcast.88, s32[1,1024]{1,0:T(1,128)} %reshape.242.live_ref, f32[128,16]{1,0:T(8,128)} %copy-done.2, f32[128,16]{1,0:T(8,128)} %multiply_add_fusion.l_ref, f32[128,1024]{1,0:T(8,128)} %copy.63.acc_ref), custom_call_target="tpu_custom_call" | custom-call | tf_op jit(solution)/shard_map/pallas_call | solution.py:63
  105.1 2.2 multiply_reduce_fusion
  107.3 0.9 convolution_convert_fusion.1
  108.3 81.0 %all_to_all.15 = bf16[32,40,1024]{2,1,0:T(8,128)(2,1)S(1)} all-to-all(bf16[32,40,1024]{2,1,0:T(8,128)(2,1)S(1)} %bitcast.85), channel_id=1, replica_groups=mesh['blk'=16,'exp'=32] {'exp'}, dimensions={0} | all-to-all | bytes 5242880 | tf_op jit(solution)/shard_map/all_to_all | solution.py:162
  189.3 2.9 %fusion.2 = f32[1280,1024]{1,0:T(8,128)S(1)} fusion(bf16[1280,1024]{1,0:T(8,128)(2,1)S(1)} %bitcast.87, bf16[1,1024,1024]{2,1,0:T(8,128)(2,1)S(1)} %copy-done), kind=kOutput, calls=%fused_computation.9 | convolution fusion | flops 2684354560 | bytes 9961472 | tf_op jit(solution)/shard_map/dot_general | solution.py:166
  192.2 3.1 %convolution_convert_fusion = bf16[1280,1024]{1,0:T(8,128)(2,1)} fusion(f32[1280,1024]{1,0:T(8,128)S(1)} %fusion.2, bf16[1,512,1024]{2,1,0:T(8,128)(2,1)S(1)} %copy-done.8), kind=kOutput, calls=%fused_computation.5 | convolution fusion | flops 1347420160 | bytes 8912896 | tf_op jit(solution)/shard_map/dot_general | solution.py:168
  195.3 6.1 %all-to-all-start.2 = ((bf16[32,40,1024]{2,1,0:T(8,128)(2,1)}), bf16[32,40,1024]{2,1,0:T(8,128)(2,1)}, u32[]{:S(2)}, u32[]{:S(2)}) async-start(bf16[32,40,1024]{2,1,0:T(8,128)(2,1)} %bitcast.86), calls=%async_computation.2 | async-start | bytes 5242880 | tf_op jit(solution)/shard_map/all_to_all | solution.py:173
  201.7 0.4 select_reduce_fusion.2
  202.5 6.6 %gather_fusion = s32[1024]{0:T(1024)S(1)} fusion(s32[128]{0:T(128)S(1)} %reshape.250, s32[1024]{0:T(1024)S(1)} %broadcast_clamp_fusion), kind=kCustom, calls=%fused_computation | custom fusion | bytes 12288 | tf_op jit(solution)/shard_map/gather | solution.py:199
  209.1 1.6 select_reduce_fusion
  210.7 3.1 %fusion.6 = bf16[1,256,1024]{2,1,0:T(8,128)(2,1)} fusion(s32[1024]{0:T(1024)S(1)} %add_select_fusion.1, s32[1024]{0:T(1024)S(1)} %gather_fusion, s32[256]{0:T(256)S(1)} %get-tuple-element.11, s32[256]{0:T(256)S(1)} %get-tuple-element.12, bf16[1,1024,1024]{2,1,0:T(8,128)(2,1)} %all-gather.2.cloned.1.call-done), kind=kOutput, calls=%fused_computation.15 | convolution fusion | flops 537919488 | bytes 2631680 | tf_op jit(solution)/shard_map/dot_general | solution.py:200
  213.9 48.5 %all-to-all-done.2 = bf16[32,40,1024]{2,1,0:T(8,128)(2,1)} async-done(((bf16[32,40,1024]{2,1,0:T(8,128)(2,1)}), bf16[32,40,1024]{2,1,0:T(8,128)(2,1)}, u32[]{:S(2)}, u32[]{:S(2)}) %all-to-all-start.2) | async-done | bytes 2621472 | tf_op jit(solution)/shard_map/all_to_all | solution.py:173
  262.4 3.7 %fusion.11 = bf16[1,128,1024]{2,1,0:T(8,128)(2,1)} fusion(f32[128,1024]{1,0:T(8,128)S(1)} %get-tuple-element.10, f32[128,1280]{1,0:T(8,128)S(1)} %select_reduce_fusion, bf16[1280,1024]{1,0:T(8,128)(2,1)} %bitcast.33), kind=kOutput, calls=%fused_computation.22 | convolution fusion | flops 2013528064 | bytes 4063232 | tf_op jit(solution)/shard_map/dot_general | solution.py:182
  (64 shorter events, 2.3 us)
Async XLA Ops:
  7.2 182.1 %copy-start = (bf16[1,1024,1024]{2,1,0:T(8,128)(2,1)S(1)}, bf16[1,1024,1024]{2,1,0:T(8,128)(2,1)}, u32[]{:S(2)}) copy-start(bf16[1,1024,1024]{2,1,0:T(8,128)(2,1)} %param.23) | copy-start | bytes 6291460
  9.7 15.4 %copy-start.5 = (s32[1,128,8]{1,2,0:T(8,128)S(1)}, s32[1,128,8]{1,2,0:T(8,128)}, u32[]{:S(2)}) copy-start(s32[1,128,8]{1,2,0:T(8,128)} %param.21) | copy-start | bytes 12292
  9.7 16.4 %copy-start.9 = (s32[1,2]{1,0:T(1,128)S(1)}, s32[1,2]{1,0:T(1,128)}, u32[]{:S(2)}) copy-start(s32[1,2]{1,0:T(1,128)} %param.18) | copy-start | bytes 28
  9.7 18.5 %copy-start.10 = (s32[1,1,4]{2,1,0:T(1,128)S(1)}, s32[1,1,4]{2,1,0:T(1,128)}, u32[]{:S(2)}) copy-start(s32[1,1,4]{2,1,0:T(1,128)} %param.19) | copy-start | bytes 52
  9.7 18.7 %copy-start.7 = (s32[1,8,1]{1,2,0:T(1,128)S(1)}, s32[1,8,1]{1,2,0:T(1,128)}, u32[]{:S(2)}) copy-start(s32[1,8,1]{1,2,0:T(1,128)} %param.25) | copy-start | bytes 100
  9.7 43.3 %copy-start.1 = (bf16[1,128,1024]{2,1,0:T(8,128)(2,1)S(1)}, bf16[1,128,1024]{2,1,0:T(8,128)(2,1)}, u32[]{:S(2)}) copy-start(bf16[1,128,1024]{2,1,0:T(8,128)(2,1)} %param.14) | copy-start | bytes 786436
  9.7 44.1 %copy-start.3 = (bf16[1,128,1024]{2,1,0:T(8,128)(2,1)S(1)}, bf16[1,128,1024]{2,1,0:T(8,128)(2,1)}, u32[]{:S(2)}) copy-start(bf16[1,128,1024]{2,1,0:T(8,128)(2,1)} %param.15) | copy-start | bytes 786436
  9.8 95.3 %all-to-all-start = ((bf16[32,32,1024]{2,1,0:T(8,128)(2,1)}), bf16[32,32,1024]{2,1,0:T(8,128)(2,1)}, u32[]{:S(2)}, u32[]{:S(2)}) async-start(bf16[32,32,1024]{2,1,0:T(8,128)(2,1)} %broadcast_in_dim.95), calls=%async_computation | async-start | bytes 4194304 | tf_op jit(solution)/shard_map/all_to_all | solution.py:38
  24.4 70.3 %all-gather.2.cloned.1.call-start = ((), (), s32[]{:S(2)}) async-start(), calls=%async_computation.3 | async-start | bytes 2228224 | tf_op jit(solution)/shard_map/all_gather | solution.py:125
  58.8 46.3 %copy-start.4 = (bf16[1,128,1024]{2,1,0:T(8,128)(2,1)S(1)}, bf16[1,128,1024]{2,1,0:T(8,128)(2,1)}, u32[]{:S(2)}) copy-start(bf16[1,128,1024]{2,1,0:T(8,128)(2,1)} %param.13) | copy-start | bytes 786436
  59.2 35.4 %copy-start.2 = (f32[128,16]{1,0:T(8,128)}, f32[128,16]{1,0:T(8,128)S(1)}, u32[]{:S(2)}) copy-start(f32[128,16]{1,0:T(8,128)S(1)} %copy.62.m_ref) | copy-start | bytes 24580
  189.3 2.9 %copy-start.8 = (bf16[1,512,1024]{2,1,0:T(8,128)(2,1)S(1)}, bf16[1,512,1024]{2,1,0:T(8,128)(2,1)}, u32[]{:S(2)}) copy-start(bf16[1,512,1024]{2,1,0:T(8,128)(2,1)} %param.24) | copy-start | bytes 3145732
  195.3 7.0 %copy-start.6 = (f32[1,128,8]{1,2,0:T(8,128)S(1)}, f32[1,128,8]{1,2,0:T(8,128)}, u32[]{:S(2)}) copy-start(f32[1,128,8]{1,2,0:T(8,128)} %param.22) | copy-start | bytes 12292
  195.3 67.1 %all-to-all-start.2 = ((bf16[32,40,1024]{2,1,0:T(8,128)(2,1)}), bf16[32,40,1024]{2,1,0:T(8,128)(2,1)}, u32[]{:S(2)}, u32[]{:S(2)}) async-start(bf16[32,40,1024]{2,1,0:T(8,128)(2,1)} %bitcast.86), calls=%async_computation.2 | async-start | bytes 5242880 | tf_op jit(solution)/shard_map/all_to_all | solution.py:173
Sparse Core Ops, SparseCore 0:
  27.3 67.3 all-gather.1

commit v8 on v2

--- a/solution.py
+++ b/solution.py
@@ -36,6 +36,27 @@
     tiles = jnp.broadcast_to(piece[None], (count,) + piece.shape)
     whole = lax.all_to_all(tiles, axis, split_axis=0, concat_axis=0, tiled=True)
     return whole.reshape((count * piece.shape[0],) + piece.shape[1:])
+
+
+def absorb_blocks(carry_state, query_heads, keys_b, values_b, visible):
+    running_max, denom, numerator = carry_state
+    scores = (
+        jnp.einsum("tkgd,nkds->tkgns", query_heads, keys_b, preferred_element_type=jnp.float32)
+        * SCALE
+    )
+    masked = jnp.where(visible, scores, NEGATIVE)
+    new_max = jnp.maximum(running_max, jnp.max(masked, axis=(-2, -1)))
+    factor = jnp.exp(running_max - new_max)
+    weight = jnp.where(visible, jnp.exp(scores - new_max[..., None, None]), 0.0)
+    denom = denom * factor + jnp.sum(weight, axis=(-2, -1))
+    added = jnp.einsum(
+        "tkgns,nkds->tkgd",
+        weight.astype(jnp.bfloat16),
+        values_b,
+        preferred_element_type=jnp.float32,
+    )
+    numerator = numerator * factor[..., None] + added
+    return (new_max, denom, numerator)
 
 
 def absorb(carry_state, query_heads, key_heads, value_heads, visible):
@@ -94,19 +115,17 @@
     keep_rows = jnp.repeat(block_keep[0], KB)
     position_abs = lax.axis_index("blk") * block_rows + jnp.arange(block_rows, dtype=jnp.int32)
     live_keys = ((keep_rows > 0) & (position_abs < prompt_lengths[0])).astype(jnp.int32)[None, :]
-    piece_kv = lax.all_gather(prompt_kv, "blk", axis=1, tiled=True)
+    local_t = prompt_kv[0].T.reshape(2, KVH, HD, block_rows)
+    blocks = lax.all_gather(local_t, "blk", axis=0, tiled=False)
     blk_count = lax.axis_size("blk")
     page_count = block_rows // PAGE
     packed = jnp.concatenate([live_keys[0], page_owner[0, :, 0]])
     packed_all = lax.all_gather(packed, "blk", axis=0, tiled=True).reshape(blk_count, -1)
     piece_live = packed_all[:, :block_rows].reshape(1, -1)
     owners_all = packed_all[:, block_rows:]
-    count = piece_kv.shape[1]
-    key_heads = piece_kv[0, :, :kv_width].reshape(count, KVH, HD)
-    value_heads = piece_kv[0, :, kv_width:].reshape(count, KVH, HD)
-    visible = (piece_live[0] > 0)[None, None, None, :]
-    running_max, denom, numerator = absorb(
-        carry_state, query_heads, key_heads, value_heads, visible
+    visible = (piece_live[0] > 0).reshape(blk_count, block_rows)[None, None, None]
+    running_max, denom, numerator = absorb_blocks(
+        carry_state, query_heads, blocks[:, 0], blocks[:, 1], visible
     )
     attended = (numerator / denom[..., None]).reshape(tok_rows, H * HD).astype(jnp.bfloat16)
     projected = jnp.dot(
@@ -164,12 +183,13 @@
     page_slot = jnp.where(owners_all == me, block_of * page_capacity + page_rank, -1).reshape(-1)
     out_rows = blk_count * page_capacity * PAGE
     row_slot = jnp.arange(out_rows, dtype=jnp.int32) // PAGE
-    prompt_rows = piece_kv.shape[1]
+    prompt_rows = blk_count * block_rows
     src_page = jnp.arange(prompt_rows, dtype=jnp.int32) // PAGE
     same_row = (jnp.arange(out_rows)[:, None] % PAGE) == (jnp.arange(prompt_rows)[None, :] % PAGE)
     chooser = (page_slot[src_page][None, :] == row_slot[:, None]) & same_row
+    prompt_full = jnp.transpose(blocks, (0, 4, 1, 2, 3)).reshape(prompt_rows, -1)
     cache_pages = jnp.dot(
-        chooser.astype(jnp.bfloat16), piece_kv[0], preferred_element_type=jnp.float32
+        chooser.astype(jnp.bfloat16), prompt_full, preferred_element_type=jnp.float32
     ).astype(jnp.bfloat16)[None]
     return (attended[None], layer_out[None], cache_pages)
 

time: 265 us -> 273 us (1.030)
  local copies, waits for them, and re-layouts: 20.7 us -> 32.1 us
  waiting for transfers between devices: 69.8 us -> 65.7 us
    all_to_all x1, waiting for transfers between devices: 46.7 us -> 31.9 us  [local(): lax.all_to_all(outgoing, 'exp', split_axis=0, concat_axis=0, tiled=True)]
    all_gather x1, waiting for transfers between devices: 22.4 us -> 33.8 us  [local(): blocks = lax.all_gather(local_t, 'blk', axis=0, tiled=False)]
    transpose x0 -> x1, local copies, waits for them, and re-layouts: none -> 7.78 us  [local(): jnp.transpose(blocks, (0, 4, 1, 2, 3)).reshape(prompt_rows, -1)]
    reshape x0 -> x1, local copies, waits for them, and re-layouts: none -> 6.49 us  [local(): jnp.transpose(blocks, (0, 4, 1, 2, 3)).reshape(prompt_rows, -1)]
    slice x5 -> x2, local copies, waits for them, and re-layouts: 5.76 us -> 0.22 us  [the longest x2 4.23 us: local(): key_heads = piece_kv[0, :, :kv_width].reshape(count, KVH, HD)]
    dot_general x1 -> x3, matrix products: 3.14 us -> 7.6 us  [the longest x1 3.14 us: local(): jnp.dot(chooser.astype(jnp.bfloat16), prompt_full, preferred_element_type...]
  transfers between devices with their start and end apart: 3 -> 3, of which waited for: 2 -> 2; matrix products, arithmetic and copies ran while one was open for 18% -> 22% of each run, Pallas kernels for 0% -> 0%
where the time goes in v8:
time: 273 us; the launch traced here: 272 us
  blocking collectives  95.2 us (35%)
  waiting for transfers between devices  65.7 us (24%)
  local copies, waits for them, and re-layouts  32.1 us (12%)
  matrix products  22 us (8%)
  starting transfers between devices  20.7 us (8%)
  other arithmetic  20.3 us (7%)
  between operations  15.8 us (6%)
    all_to_all x1, blocking collectives, local(): lax.all_to_all(dispatch, 'exp', split_axis=0, concat_axis=0, tiled=True)  80 us
    all_gather x1, waiting for transfers between devices, local(): blocks = lax.all_gather(local_t, 'blk', axis=0, tiled=False)  33.8 us
    all_to_all x1, waiting for transfers between devices, local(): lax.all_to_all(outgoing, 'exp', split_axis=0, concat_axis=0, tiled=True)  31.9 us
    unnamed x1, blocking collectives  15.2 us
    all_to_all x1, starting transfers between devices, gather_rows(): whole = lax.all_to_all(tiles, axis, split_axis=0, concat_axis=0, tiled=True)  14.6 us
    another operation x4, other arithmetic  9.33 us
    transpose x1, local copies, waits for them, and re-layouts, local(): jnp.transpose(blocks, (0, 4, 1, 2, 3)).reshape(prompt_rows, -1)  7.78 us
    gather x1, local copies, waits for them, and re-layouts, local(): chooser = (page_slot[src_page][None, :] == row_slot[:, None]) & same_row  6.57 us
  transfers between devices with their start and end apart: 3, of which 2 were waited for; matrix products, arithmetic and copies ran while one was open for 22% of the time, Pallas kernels for 0%

profile of v8, /device:TPU:1, one launch (start us, length us, event | category | flops | bytes accessed | tf_op | source)
XLA Modules:
  0.0 271.8 jit_solution(16050725092797568787)
XLA Ops:
  7.2 1.3 all_gather_reshape.3
  8.5 0.8 copy.46
  9.3 2.4 broadcast_in_dim.110
  11.8 14.6 %all-to-all-start = ((bf16[32,32,1024]{2,1,0:T(8,128)(2,1)}), bf16[32,32,1024]{2,1,0:T(8,128)(2,1)}, u32[]{:S(2)}, u32[]{:S(2)}) async-start(bf16[32,32,1024]{2,1,0:T(8,128)(2,1)} %broadcast_in_dim.110), calls=%async_computation | async-start | bytes 4194304 | tf_op jit(solution)/shard_map/all_to_all | solution.py:37
  27.6 1.3 dynamic-slice
  29.7 15.2 %all-reduce = s32[1152]{0:T(1024)S(1)} all-reduce(s32[1152]{0:T(1024)S(1)} %add_dynamic-update-slice_fusion), channel_id=1, replica_groups=mesh['blk'=16,'exp'=32] {'blk'}, use_global_device_ids=true, to_apply=%add | all-reduce | flops 1152 | bytes 9216
  45.4 0.8 copy.42
  46.2 0.8 copy.44
  46.9 9.0 %reduce-window.19 = s32[32,8,128]{2,1,0:T(8,128)S(1)} reduce-window(s32[32,8,128]{2,1,0:T(8,128)S(1)} %fusion.46, s32[]{:T(128)} %constant.83.clone.1), window={size=1x1x128 pad=0_0x0_0x127_0}, to_apply=%region_6.7 | reduce-window | flops 4161536 | bytes 262148 | tf_op jit(solution)/shard_map/reduce-window.1
  56.5 0.6 copy-done.8
  57.3 5.3 %fusion.5 = pred[1280,128]{1,0:T(8,128)(4,1)} fusion(s32[128,8]{0,1:T(8,128)S(1)} %copy.55), kind=kLoop, calls=%fused_computation.11 | loop fusion | flops 2457600 | bytes 167936 | tf_op jit(solution)/shard_map/reduce_or | solution.py:149
  62.7 1.3 select_reduce_fusion.1
  64.0 33.8 %all-gather.2.cloned.1.call-done = bf16[16,2,8,64,64]{3,4,0,2,1:T(8,128)(2,1)} async-done(((bf16[1,2,8,64,64]{3,4,0,2,1:T(8,128)(2,1)}), bf16[16,2,8,64,64]{3,4,0,2,1:T(8,128)(2,1)}) %all-gather.2.cloned.1.call-update) | async-done | bytes 2097168 | tf_op jit(solution)/shard_map/all_gather | solution.py:119
  97.8 2.7 fusion
  100.7 1.8 fusion.3
  102.9 1.8 fusion.15
  105.1 2.2 multiply_reduce_fusion
  107.3 0.9 convolution_convert_fusion.1
  108.2 80.0 %all_to_all.15 = bf16[32,40,1024]{2,1,0:T(8,128)(2,1)S(1)} all-to-all(bf16[32,40,1024]{2,1,0:T(8,128)(2,1)S(1)} %bitcast.142), channel_id=1, replica_groups=mesh['blk'=16,'exp'=32] {'exp'}, dimensions={0} | all-to-all | bytes 5242880 | tf_op jit(solution)/shard_map/all_to_all | solution.py:152
  188.2 2.9 %fusion.11 = f32[1280,1024]{1,0:T(8,128)S(1)} fusion(bf16[1280,1024]{1,0:T(8,128)(2,1)S(1)} %bitcast.145, bf16[1,1024,1024]{2,1,0:T(8,128)(2,1)S(1)} %copy-done), kind=kOutput, calls=%fused_computation.21 | convolution fusion | flops 2684354560 | bytes 9961472 | tf_op jit(solution)/shard_map/dot_general | solution.py:156
  191.1 3.2 %convolution_convert_fusion = bf16[1280,1024]{1,0:T(8,128)(2,1)} fusion(f32[1280,1024]{1,0:T(8,128)S(1)} %fusion.11, bf16[1,512,1024]{2,1,0:T(8,128)(2,1)S(1)} %copy-done.13), kind=kOutput, calls=%fused_computation.14 | convolution fusion | flops 1347420160 | bytes 8912896 | tf_op jit(solution)/shard_map/dot_general | solution.py:158
  194.2 6.0 %all-to-all-start.2 = ((bf16[32,40,1024]{2,1,0:T(8,128)(2,1)}), bf16[32,40,1024]{2,1,0:T(8,128)(2,1)}, u32[]{:S(2)}, u32[]{:S(2)}) async-start(bf16[32,40,1024]{2,1,0:T(8,128)(2,1)} %bitcast.144), calls=%async_computation.2 | async-start | bytes 5242880 | tf_op jit(solution)/shard_map/all_to_all | solution.py:163
  200.4 0.7 copy.54
  201.3 0.4 select_reduce_fusion.2
  202.0 6.6 %gather_fusion = s32[1024]{0:T(1024)S(1)} fusion(s32[128]{0:T(128)S(1)} %reshape.279, s32[1024]{0:T(1024)S(1)} %broadcast_clamp_fusion), kind=kCustom, calls=%fused_computation | custom fusion | bytes 12288 | tf_op jit(solution)/shard_map/gather | solution.py:189
  208.6 2.5 select_reduce_fusion
  211.1 0.9 copy.57
  211.9 7.8 %copy.56 = bf16[16,64,2,8,64]{4,3,2,1,0:T(8,128)(2,1)} copy(bf16[16,64,2,8,64]{4,1,0,3,2:T(8,128)(2,1)} %bitcast.143) | data formatting | bytes 4194304 | tf_op jit(solution)/shard_map/transpose | solution.py:190
  219.7 6.5 %reshape.280 = bf16[1024,1024]{1,0:T(8,128)(2,1)} reshape(bf16[16,64,2,8,64]{4,3,2,1,0:T(8,128)(2,1)} %copy.56) | data formatting | bytes 4194304 | tf_op jit(solution)/shard_map/reshape | solution.py:190
  226.2 3.1 %fusion.18 = bf16[1,256,1024]{2,1,0:T(8,128)(2,1)} fusion(bf16[1024,1024]{1,0:T(8,128)(2,1)} %reshape.280, s32[1024]{0:T(1024)S(1)} %add_select_fusion.1, s32[1024]{0:T(1024)S(1)} %gather_fusion, s32[256]{0:T(256)S(1)} %get-tuple-element.25, s32[256]{0:T(256)S(1)} %get-tuple-element.26), kind=kOutput, calls=%fused_computation.28 | convolution fusion | flops 537919488 | bytes 2631680 | tf_op jit(solution)/shard_map/dot_general | solution.py:191
  229.4 31.9 %all-to-all-done.2 = bf16[32,40,1024]{2,1,0:T(8,128)(2,1)} async-done(((bf16[32,40,1024]{2,1,0:T(8,128)(2,1)}), bf16[32,40,1024]{2,1,0:T(8,128)(2,1)}, u32[]{:S(2)}, u32[]{:S(2)}) %all-to-all-start.2) | async-done | bytes 2621472 | tf_op jit(solution)/shard_map/all_to_all | solution.py:163
  261.2 3.7 %fusion.27 = bf16[1,128,1024]{2,1,0:T(8,128)(2,1)} fusion(f32[128,1024]{1,0:T(8,128)S(1)} %get-tuple-element.24, f32[128,1280]{1,0:T(8,128)S(1)} %select_reduce_fusion, bf16[1280,1024]{1,0:T(8,128)(2,1)} %bitcast.42), kind=kOutput, calls=%fused_computation.39 | convolution fusion | flops 2013528064 | bytes 4063232 | tf_op jit(solution)/shard_map/dot_general | solution.py:172
  (78 shorter events, 3.5 us)
Async XLA Ops:
  7.2 181.0 %copy-start = (bf16[1,1024,1024]{2,1,0:T(8,128)(2,1)S(1)}, bf16[1,1024,1024]{2,1,0:T(8,128)(2,1)}, u32[]{:S(2)}) copy-start(bf16[1,1024,1024]{2,1,0:T(8,128)(2,1)} %param.23) | copy-start | bytes 6291460
  7.2 90.6 %all-gather.2.cloned.1.call-start = ((), (), s32[]{:S(2)}) async-start(), calls=%async_computation.3 | async-start | bytes 4456448 | tf_op jit(solution)/shard_map/all_gather | solution.py:119
  11.7 14.7 %copy-start.10 = (s32[1,128,8]{1,2,0:T(8,128)S(1)}, s32[1,128,8]{1,2,0:T(8,128)}, u32[]{:S(2)}) copy-start(s32[1,128,8]{1,2,0:T(8,128)} %param.21) | copy-start | bytes 12292
  11.7 15.0 %copy-start.14 = (s32[1,2]{1,0:T(1,128)S(1)}, s32[1,2]{1,0:T(1,128)}, u32[]{:S(2)}) copy-start(s32[1,2]{1,0:T(1,128)} %param.18) | copy-start | bytes 28
  11.7 17.8 %copy-start.12 = (s32[1,8,1]{1,2,0:T(1,128)S(1)}, s32[1,8,1]{1,2,0:T(1,128)}, u32[]{:S(2)}) copy-start(s32[1,8,1]{1,2,0:T(1,128)} %param.25) | copy-start | bytes 100
  11.7 33.3 %copy-start.3 = (bf16[1,128,1024]{2,1,0:T(8,128)(2,1)S(1)}, bf16[1,128,1024]{2,1,0:T(8,128)(2,1)}, u32[]{:S(2)}) copy-start(bf16[1,128,1024]{2,1,0:T(8,128)(2,1)} %param.14) | copy-start | bytes 786436
  11.7 33.5 %copy-start.15 = (s32[1,1,4]{2,1,0:T(1,128)S(1)}, s32[1,1,4]{2,1,0:T(1,128)}, u32[]{:S(2)}) copy-start(s32[1,1,4]{2,1,0:T(1,128)} %param.19) | copy-start | bytes 52
  11.8 33.6 %copy-start.4 = (bf16[1,128,1024]{2,1,0:T(8,128)(2,1)S(1)}, bf16[1,128,1024]{2,1,0:T(8,128)(2,1)}, u32[]{:S(2)}) copy-start(bf16[1,128,1024]{2,1,0:T(8,128)(2,1)} %param.15) | copy-start | bytes 786436
  11.8 93.3 %all-to-all-start = ((bf16[32,32,1024]{2,1,0:T(8,128)(2,1)}), bf16[32,32,1024]{2,1,0:T(8,128)(2,1)}, u32[]{:S(2)}, u32[]{:S(2)}) async-start(bf16[32,32,1024]{2,1,0:T(8,128)(2,1)} %broadcast_in_dim.110), calls=%async_computation | async-start | bytes 4194304 | tf_op jit(solution)/shard_map/all_to_all | solution.py:37
  45.0 17.7 %copy-start.5 = (s32[16,72]{1,0:T(8,128)}, s32[16,72]{1,0:T(8,128)S(1)}, u32[]{:S(2)}) copy-start(s32[16,72]{1,0:T(8,128)S(1)} %reshape.274) | copy-start | bytes 13828
  56.5 0.6 copy-start.8
  100.7 2.2 copy-start.1
  102.9 1.8 copy-start.7
  105.0 2.2 copy-start.2
  188.1 2.9 %copy-start.13 = (bf16[1,512,1024]{2,1,0:T(8,128)(2,1)S(1)}, bf16[1,512,1024]{2,1,0:T(8,128)(2,1)}, u32[]{:S(2)}) copy-start(bf16[1,512,1024]{2,1,0:T(8,128)(2,1)} %param.24) | copy-start | bytes 3145732
  194.2 6.0 %copy-start.9 = (s32[1024]{0:T(1024)S(1)}, s32[1024]{0:T(1024)}, u32[]{:S(2)}) copy-start(s32[1024]{0:T(1024)} %copy-done.8) | copy-start | bytes 12292
  194.2 6.1 %copy-start.6 = (s32[16,72]{1,0:T(8,128)S(1)}, s32[16,72]{1,0:T(8,128)}, u32[]{:S(2)}) copy-start(s32[16,72]{1,0:T(8,128)} %copy-done.5) | copy-start | bytes 13828
  194.2 6.2 %copy-start.11 = (f32[1,128,8]{1,2,0:T(8,128)S(1)}, f32[1,128,8]{1,2,0:T(8,128)}, u32[]{:S(2)}) copy-start(f32[1,128,8]{1,2,0:T(8,128)} %param.22) | copy-start | bytes 12292
  194.2 67.0 %all-to-all-start.2 = ((bf16[32,40,1024]{2,1,0:T(8,128)(2,1)}), bf16[32,40,1024]{2,1,0:T(8,128)(2,1)}, u32[]{:S(2)}, u32[]{:S(2)}) async-start(bf16[32,40,1024]{2,1,0:T(8,128)(2,1)} %bitcast.144), calls=%async_computation.2 | async-start | bytes 5242880 | tf_op jit(solution)/shard_map/all_to_all | solution.py:163
Sparse Core Ops, SparseCore 0:
  10.7 87.0 all-gather.1

commit v9 on v2

--- a/solution.py
+++ b/solution.py
@@ -153,7 +153,7 @@
     combined = jnp.dot(
         slot_weight,
         returned.reshape(experts * capacity, D).astype(jnp.float32),
-        precision=lax.Precision.HIGHEST,
+        precision=lax.Precision.HIGH,
         preferred_element_type=jnp.float32,
     )
     layer_out = (stream_f32 + combined).astype(jnp.bfloat16)

time: 265 us -> 264 us (level)
  no operation moved by 1% of the time
where the time goes in v9:
time: 264 us; the launch traced here: 263 us
  blocking collectives  95.7 us (36%)
  waiting for transfers between devices  69.8 us (26%)
  matrix products  20.9 us (8%)
  local copies, waits for them, and re-layouts  20.7 us (8%)
  starting transfers between devices  20.7 us (8%)
  other arithmetic  19.9 us (8%)
  between operations  15.8 us (6%)
    all_to_all x1, blocking collectives, local(): lax.all_to_all(dispatch, 'exp', split_axis=0, concat_axis=0, tiled=True)  81 us
    all_to_all x1, waiting for transfers between devices, local(): lax.all_to_all(outgoing, 'exp', split_axis=0, concat_axis=0, tiled=True)  46.7 us
    all_gather x1, waiting for transfers between devices, local(): piece_kv = lax.all_gather(prompt_kv, 'blk', axis=1, tiled=True)  22.4 us
    unnamed x1, blocking collectives  14.7 us
    all_to_all x1, starting transfers between devices, gather_rows(): whole = lax.all_to_all(tiles, axis, split_axis=0, concat_axis=0, tiled=True)  14.6 us
    another operation x4, other arithmetic  9.33 us
    gather x1, local copies, waits for them, and re-layouts, local(): chooser = (page_slot[src_page][None, :] == row_slot[:, None]) & same_row  6.57 us
    all_to_all x1, starting transfers between devices, local(): lax.all_to_all(outgoing, 'exp', split_axis=0, concat_axis=0, tiled=True)  6 us
  transfers between devices with their start and end apart: 3, of which 2 were waited for; matrix products, arithmetic and copies ran while one was open for 18% of the time, Pallas kernels for 0%

profile of v9, /device:TPU:1, one launch (start us, length us, event | category | flops | bytes accessed | tf_op | source)
XLA Modules:
  0.0 263.4 jit_solution(6552238439701241968)
XLA Ops:
  7.2 0.7 all-gather.2.cloned.1.call-update
  7.9 2.4 broadcast_in_dim.111
  10.3 14.6 %all-to-all-start = ((bf16[32,32,1024]{2,1,0:T(8,128)(2,1)}), bf16[32,32,1024]{2,1,0:T(8,128)(2,1)}, u32[]{:S(2)}, u32[]{:S(2)}) async-start(bf16[32,32,1024]{2,1,0:T(8,128)(2,1)} %broadcast_in_dim.111), calls=%async_computation | async-start | bytes 4194304 | tf_op jit(solution)/shard_map/all_to_all | solution.py:37
  26.1 1.3 dynamic-slice
  28.3 14.7 %all-reduce = s32[1152]{0:T(1024)S(1)} all-reduce(s32[1152]{0:T(1024)S(1)} %add_dynamic-update-slice_fusion), channel_id=1, replica_groups=mesh['blk'=16,'exp'=32] {'blk'}, use_global_device_ids=true, to_apply=%add | all-reduce | flops 1152 | bytes 9216
  43.7 0.8 copy.44
  44.4 9.0 %reduce-window.19 = s32[32,8,128]{2,1,0:T(8,128)S(1)} reduce-window(s32[32,8,128]{2,1,0:T(8,128)S(1)} %fusion.52, s32[]{:T(128)} %constant.83.clone.1), window={size=1x1x128 pad=0_0x0_0x127_0}, to_apply=%region_6.7 | reduce-window | flops 4161536 | bytes 262148 | tf_op jit(solution)/shard_map/reduce-window.1
  54.2 5.3 %fusion.5 = pred[1280,128]{1,0:T(8,128)(4,1)} fusion(s32[128,8]{0,1:T(8,128)S(1)} %copy.55), kind=kLoop, calls=%fused_computation.11 | loop fusion | flops 2457600 | bytes 167936 | tf_op jit(solution)/shard_map/reduce_or | solution.py:130
  59.6 1.3 select_reduce_fusion.1
  60.9 22.4 %all-gather.2.cloned.1.call-done = bf16[1,1024,1024]{2,1,0:T(8,128)(2,1)} async-done(((bf16[1,64,1024]{2,1,0:T(8,128)(2,1)}), bf16[1,1024,1024]{2,1,0:T(8,128)(2,1)}) %all-gather.2.cloned.1.call-update) | async-done | bytes 2097168 | tf_op jit(solution)/shard_map/all_gather | solution.py:97
  83.3 2.7 %fusion.65 = (bf16[1,1024,512]{2,1,0:T(8,128)(2,1)}, bf16[1,1024,512]{2,1,0:T(8,128)(2,1)S(1)}) fusion(bf16[1,1024,1024]{2,1,0:T(8,128)(2,1)} %all-gather.2.cloned.1.call-done), kind=kLoop, calls=%fused_computation.108 | loop fusion | bytes 4194304 | tf_op jit(solution)/shard_map/slice | solution.py:105
  86.1 1.3 copy.47
  87.4 1.5 copy.46
  88.9 2.2 fusion
  91.1 0.2 fusion.38
  91.3 2.2 fusion.3
  93.6 1.5 fusion.22
  95.2 0.3 fusion.30
  95.5 0.6 copy-done.7
  96.1 2.1 multiply_reduce_fusion
  98.3 0.9 convolution_convert_fusion.1
  99.2 81.0 %all_to_all.15 = bf16[32,40,1024]{2,1,0:T(8,128)(2,1)S(1)} all-to-all(bf16[32,40,1024]{2,1,0:T(8,128)(2,1)S(1)} %bitcast.124), channel_id=1, replica_groups=mesh['blk'=16,'exp'=32] {'exp'}, dimensions={0} | all-to-all | bytes 5242880 | tf_op jit(solution)/shard_map/all_to_all | solution.py:133
  180.2 2.9 %fusion.12 = f32[1280,1024]{1,0:T(8,128)S(1)} fusion(bf16[1280,1024]{1,0:T(8,128)(2,1)S(1)} %bitcast.127, bf16[1,1024,1024]{2,1,0:T(8,128)(2,1)S(1)} %copy-done), kind=kOutput, calls=%fused_computation.20 | convolution fusion | flops 2684354560 | bytes 9961472 | tf_op jit(solution)/shard_map/dot_general | solution.py:137
  183.1 3.1 %convolution_convert_fusion = bf16[1280,1024]{1,0:T(8,128)(2,1)} fusion(f32[1280,1024]{1,0:T(8,128)S(1)} %fusion.12, bf16[1,512,1024]{2,1,0:T(8,128)(2,1)S(1)} %copy-done.12), kind=kOutput, calls=%fused_computation.14 | convolution fusion | flops 1347420160 | bytes 8912896 | tf_op jit(solution)/shard_map/dot_general | solution.py:139
  186.3 6.0 %all-to-all-start.2 = ((bf16[32,40,1024]{2,1,0:T(8,128)(2,1)}), bf16[32,40,1024]{2,1,0:T(8,128)(2,1)}, u32[]{:S(2)}, u32[]{:S(2)}) async-start(bf16[32,40,1024]{2,1,0:T(8,128)(2,1)} %bitcast.126), calls=%async_computation.2 | async-start | bytes 5242880 | tf_op jit(solution)/shard_map/all_to_all | solution.py:144
  192.7 0.4 select_reduce_fusion.2
  193.3 6.6 %gather_fusion = s32[1024]{0:T(1024)S(1)} fusion(s32[128]{0:T(128)S(1)} %reshape.278, s32[1024]{0:T(1024)S(1)} %broadcast_clamp_fusion), kind=kCustom, calls=%fused_computation | custom fusion | bytes 12288 | tf_op jit(solution)/shard_map/gather | solution.py:170
  199.9 1.6 select_reduce_fusion
  201.6 1.8 copy.56
  203.4 3.1 %fusion.19 = bf16[1,256,1024]{2,1,0:T(8,128)(2,1)} fusion(bf16[1,1024,1024]{2,1,0:T(8,128)(2,1)} %all-gather.2.cloned.1.call-done, s32[1024]{0:T(1024)S(1)} %add_select_fusion.1, s32[1024]{0:T(1024)S(1)} %gather_fusion, s32[256]{0:T(256)S(1)} %get-tuple-element.27, s32[256]{0:T(256)S(1)} %get-tuple-element.28), kind=kOutput, calls=%fused_computation.26 | convolution fusion | flops 537919488 | bytes 2631680 | tf_op jit(solution)/shard_map/dot_general | solution.py:171
  206.5 46.7 %all-to-all-done.2 = bf16[32,40,1024]{2,1,0:T(8,128)(2,1)} async-done(((bf16[32,40,1024]{2,1,0:T(8,128)(2,1)}), bf16[32,40,1024]{2,1,0:T(8,128)(2,1)}, u32[]{:S(2)}, u32[]{:S(2)}) %all-to-all-start.2) | async-done | bytes 2621472 | tf_op jit(solution)/shard_map/all_to_all | solution.py:144
  253.3 3.3 %fusion.33 = bf16[1,128,1024]{2,1,0:T(8,128)(2,1)} fusion(f32[128,1024]{1,0:T(8,128)S(1)} %get-tuple-element.26, f32[128,1280]{1,0:T(8,128)S(1)} %select_reduce_fusion, bf16[1280,1024]{1,0:T(8,128)(2,1)} %bitcast.37), kind=kOutput, calls=%fused_computation.38 | convolution fusion | flops 1006895104 | bytes 4063232 | tf_op jit(solution)/shard_map/dot_general | solution.py:153
  (76 shorter events, 2.9 us)
Async XLA Ops:
  7.2 173.0 %copy-start = (bf16[1,1024,1024]{2,1,0:T(8,128)(2,1)S(1)}, bf16[1,1024,1024]{2,1,0:T(8,128)(2,1)}, u32[]{:S(2)}) copy-start(bf16[1,1024,1024]{2,1,0:T(8,128)(2,1)} %param.23) | copy-start | bytes 6291460
  7.2 76.1 %all-gather.2.cloned.1.call-start = ((), (), s32[]{:S(2)}) async-start(), calls=%async_computation.3 | async-start | bytes 2228224 | tf_op jit(solution)/shard_map/all_gather | solution.py:97
  10.3 14.7 %copy-start.9 = (s32[1,128,8]{1,2,0:T(8,128)S(1)}, s32[1,128,8]{1,2,0:T(8,128)}, u32[]{:S(2)}) copy-start(s32[1,128,8]{1,2,0:T(8,128)} %param.21) | copy-start | bytes 12292
  10.3 15.0 %copy-start.13 = (s32[1,2]{1,0:T(1,128)S(1)}, s32[1,2]{1,0:T(1,128)}, u32[]{:S(2)}) copy-start(s32[1,2]{1,0:T(1,128)} %param.18) | copy-start | bytes 28
  10.3 17.8 %copy-start.11 = (s32[1,8,1]{1,2,0:T(1,128)S(1)}, s32[1,8,1]{1,2,0:T(1,128)}, u32[]{:S(2)}) copy-start(s32[1,8,1]{1,2,0:T(1,128)} %param.25) | copy-start | bytes 100
  10.3 32.8 %copy-start.5 = (bf16[1,128,1024]{2,1,0:T(8,128)(2,1)S(1)}, bf16[1,128,1024]{2,1,0:T(8,128)(2,1)}, u32[]{:S(2)}) copy-start(bf16[1,128,1024]{2,1,0:T(8,128)(2,1)} %param.14) | copy-start | bytes 786436
  10.3 33.0 %copy-start.14 = (s32[1,1,4]{2,1,0:T(1,128)S(1)}, s32[1,1,4]{2,1,0:T(1,128)}, u32[]{:S(2)}) copy-start(s32[1,1,4]{2,1,0:T(1,128)} %param.19) | copy-start | bytes 52
  10.3 33.2 %copy-start.6 = (bf16[1,128,1024]{2,1,0:T(8,128)(2,1)S(1)}, bf16[1,128,1024]{2,1,0:T(8,128)(2,1)}, u32[]{:S(2)}) copy-start(bf16[1,128,1024]{2,1,0:T(8,128)(2,1)} %param.15) | copy-start | bytes 786436
  10.3 85.2 %all-to-all-start = ((bf16[32,32,1024]{2,1,0:T(8,128)(2,1)}), bf16[32,32,1024]{2,1,0:T(8,128)(2,1)}, u32[]{:S(2)}, u32[]{:S(2)}) async-start(bf16[32,32,1024]{2,1,0:T(8,128)(2,1)} %broadcast_in_dim.111), calls=%async_computation | async-start | bytes 4194304 | tf_op jit(solution)/shard_map/all_to_all | solution.py:37
  88.9 2.2 copy-start.1
  91.3 2.3 copy-start.2
  93.6 1.6 copy-start.8
  95.2 1.0 copy-start.7
  95.2 3.1 %copy-start.4 = (pred[1280,128]{1,0:T(8,128)(4,1)S(1)}, pred[1280,128]{1,0:T(8,128)(4,1)}, u32[]{:S(2)}) copy-start(pred[1280,128]{1,0:T(8,128)(4,1)} %fusion.5) | copy-start | bytes 491524
  95.5 3.7 %copy-start.3 = (bf16[128,8,2,64]{0,3,2,1:T(8,128)(2,1)}, bf16[128,8,2,64]{0,3,2,1:T(8,128)(2,1)S(1)}, u32[]{:S(2)}) copy-start(bf16[128,8,2,64]{0,3,2,1:T(8,128)(2,1)S(1)} %fusion.30) | copy-start | bytes 786436
  180.2 2.9 %copy-start.12 = (bf16[1,512,1024]{2,1,0:T(8,128)(2,1)S(1)}, bf16[1,512,1024]{2,1,0:T(8,128)(2,1)}, u32[]{:S(2)}) copy-start(bf16[1,512,1024]{2,1,0:T(8,128)(2,1)} %param.24) | copy-start | bytes 3145732
  186.2 6.2 %copy-start.10 = (f32[1,128,8]{1,2,0:T(8,128)S(1)}, f32[1,128,8]{1,2,0:T(8,128)}, u32[]{:S(2)}) copy-start(f32[1,128,8]{1,2,0:T(8,128)} %param.22) | copy-start | bytes 12292
  186.3 67.0 %all-to-all-start.2 = ((bf16[32,40,1024]{2,1,0:T(8,128)(2,1)}), bf16[32,40,1024]{2,1,0:T(8,128)(2,1)}, u32[]{:S(2)}, u32[]{:S(2)}) async-start(bf16[32,40,1024]{2,1,0:T(8,128)(2,1)} %bitcast.126), calls=%async_computation.2 | async-start | bytes 5242880 | tf_op jit(solution)/shard_map/all_to_all | solution.py:144
Sparse Core Ops, SparseCore 0:
  10.1 73.1 all-gather.1
